TPU v7x, 32 devices: a whole 2x2x4 slice. The times are simulated.
32 devices in a mesh: group: 2 (over x), sector: 16 (over z, y, core).
Axes of the slice: x: 2, y: 2, z: 4, core: 2. Of those that a mesh axis runs over, the one named last changes fastest.
Arguments:
- wave: bfloat16 [32, 16, 256, 256], P(('group', 'sector')), parts along dimension 0, may hold values from -6 to 6
- left_ops: bfloat16 [384, 256, 256], P(('group', 'sector')), parts along dimension 0, may hold values from -0.375 to 0.375
- right_ops: bfloat16 [384, 256, 256], P(('group', 'sector')), parts along dimension 0, may hold values from -0.375 to 0.375
- deltas: int32 [384], P(('group', 'sector')), parts along dimension 0, may hold values from -1 to 1, as said below
- counts: int32 [32], P(('group', 'sector')), parts along dimension 0, may hold values from 2 to 12, as said below
Outputs:
- sigma: bfloat16 [32, 16, 256, 256], P(('group', 'sector')), parts along dimension 0
There are 2 independent parts, one for each index of `group`. A program takes and returns all parts, laid end to end along the dimension named above; each array names one. Nothing has to cross between parts.
Inputs may be any that keep to these rules, and one draw needn't show every extreme that they name: `counts`: some sector has exactly 12 live slots in every draw; slots at or beyond a sector's count are unused. Every sector has 2 or more live slots. In each aligned pair of sectors 2i and 2i + 1 at most one has more than 6 live slots, and every other sector has 2 or 3 live slots. `deltas`: slot 0 of every sector reads the sector below it (offset -1) and slot 1 the sector above it (offset +1).
All inputs are finite; a program needn't handle non-finite values.
Results may differ from a plain program's by a relative error of at most 0.0049.
Values may be sent and summed in bfloat16 or wider, within the bound.
No kernel may reach another device: no remote copies, remote signals or barrier semaphores. Data moves between devices by JAX's collectives and lax.ppermute only.
A program may use at most 64 MiB of HBM per device.

v0:
```python
import jax
import jax.numpy as jnp
from jax import lax
from jax.sharding import PartitionSpec as P


def extended(cells, sides, width):
    for axis, dim in sides:
        count = lax.axis_size(axis)
        ends = count - 1
        head = lax.slice_in_dim(cells, 0, width, axis=dim)
        tail = lax.slice_in_dim(cells, cells.shape[dim] - width, cells.shape[dim], axis=dim)
        cells = jnp.concatenate(
            [
                lax.ppermute(tail, axis, [(i, (i + 1) % count) for i in range(ends)]),
                cells,
                lax.ppermute(head, axis, [((i + 1) % count, i) for i in range(ends)]),
            ],
            axis=dim,
        )
    return cells


def apply_pairs(sources, left_ops, right_ops, deltas, offset, last_slot):
    roots_here = sources.shape[1]
    width = sources.shape[2]

    def add_pair(slot_index, running):
        where_from = deltas[slot_index] + offset
        source_block = lax.dynamic_index_in_dim(sources, where_from, 0, keepdims=False)
        left_op = lax.dynamic_index_in_dim(left_ops, slot_index, 0, keepdims=False)
        right_op = lax.dynamic_index_in_dim(right_ops, slot_index, 0, keepdims=False)
        mixed = jnp.einsum(
            "ij,rjk->rik", left_op, source_block, preferred_element_type=jnp.float32
        ).astype(jnp.bfloat16)
        return running + jnp.einsum(
            "rik,lk->ril", mixed, right_op, preferred_element_type=jnp.float32
        )

    empty = jnp.zeros((roots_here, width, width), jnp.float32)
    return lax.fori_loop(jnp.int32(0), last_slot, add_pair, empty)


def on_device(wave, left_ops, right_ops, deltas, counts):
    sources = extended(wave, (("sector", 0),), 1)
    own_count = counts[0]
    running = apply_pairs(sources, left_ops, right_ops, deltas, 1, own_count)
    return running.astype(jnp.bfloat16)[None]


def solution(mesh):
    return jax.shard_map(
        on_device,
        mesh=mesh,
        in_specs=(
            P(("group", "sector"), None, None, None),
            P(("group", "sector"), None, None),
            P(("group", "sector"), None, None),
            P(("group", "sector")),
            P(("group", "sector")),
        ),
        out_specs=P(("group", "sector"), None, None, None),
        check_vma=False,
    )
```

profile of v0, /device:TPU:17, one launch (start us, length us, event | category | flops | bytes accessed | tf_op | source)
XLA Modules:
  0.0 166.2 jit_solution(6876253183321466080)
XLA Ops:
  0.0 3.7 %collective-permute-start = (bf16[1,16,256,256]{3,2,1,0:T(8,128)(2,1)}, bf16[1,16,256,256]{3,2,1,0:T(8,128)(2,1)S(1)}, u32[]{:S(2)}, u32[]{:S(2)}) collective-permute-start(bf16[1,16,256,256]{3,2,1,0:T(8,128)(2,1)} %param.7), channel_id=1, source_target_pairs={{0,1},{1,2},{2,3},{3,4},{4,5},{5,6},{6,7},{7,8},{8,9},{9,10},{10,1... | collective-permute-start | bytes 6291464 | tf_op jit(solution)/shard_map/ppermute | solution.py:15
  3.7 1.9 %collective-permute-start.1 = (bf16[1,16,256,256]{3,2,1,0:T(8,128)(2,1)}, bf16[1,16,256,256]{3,2,1,0:T(8,128)(2,1)}, u32[]{:S(2)}, u32[]{:S(2)}) collective-permute-start(bf16[1,16,256,256]{3,2,1,0:T(8,128)(2,1)} %param.7), channel_id=1, source_target_pairs={{1,0},{2,1},{3,2},{4,3},{5,4},{6,5},{7,6},{8,7},{9,8},{10,9},{11,1... | collective-permute-start | bytes 6291464 | tf_op jit(solution)/shard_map/ppermute | solution.py:17
  5.6 43.8 %collective-permute-done = bf16[1,16,256,256]{3,2,1,0:T(8,128)(2,1)S(1)} collective-permute-done((bf16[1,16,256,256]{3,2,1,0:T(8,128)(2,1)}, bf16[1,16,256,256]{3,2,1,0:T(8,128)(2,1)S(1)}, u32[]{:S(2)}, u32[]{:S(2)}) %collective-permute-start) | collective-permute-done | bytes 2097184 | tf_op jit(solution)/shard_map/ppermute | solution.py:15
  49.4 1.6 collective-permute-done.1
  51.0 5.5 %pad_maximum_fusion = bf16[3,16,256,256]{3,2,1,0:T(8,128)(2,1)} fusion(bf16[1,16,256,256]{3,2,1,0:T(8,128)(2,1)} %collective-permute-done.1, bf16[1,16,256,256]{3,2,1,0:T(8,128)(2,1)} %param.7, bf16[1,16,256,256]{3,2,1,0:T(8,128)(2,1)S(1)} %collective-permute-done), kind=kLoop, calls=%fused_computation.11 | loop fusion | flops 6291456 | bytes 12582912 | tf_op jit(solution)/shard_map/concatenate | solution.py:13
  56.5 2.5 %broadcast_in_dim.6 = f32[16,256,256]{2,1,0:T(8,128)} broadcast(f32[]{:T(128)} %constant.37.clone.1), dimensions={} | broadcast | bytes 4194308 | tf_op jit(solution)/shard_map/broadcast_in_dim | solution.py:40
  59.0 103.5 %while.12 = (s32[]{:T(128)}, f32[16,256,256]{2,1,0:T(8,128)}, s32[]{:T(128)}, s32[12]{0:T(128)S(1)}, bf16[3,16,256,256]{3,2,1,0:T(8,128)(2,1)}, /*index=5*/bf16[...) while((s32[]{:T(128)}, f32[16,256,256]{2,1,0:T(8,128)}, ...), condition=%wide.region_1.2_spmd, body=%wide.region_0.1_spmd.sunk | while | flops 1075838976 | bytes 10749657 | solution.py:41
  59.6 0.6 dynamic_slice.47
  61.4 6.2 %convolution_add_fusion.2 = f32[16,256,256]{2,1,0:T(8,128)} fusion(f32[16,256,256]{2,1,0:T(8,128)} %get-tuple-element.169, bf16[3,16,256,256]{3,2,1,0:T(8,128)(2,1)} %get-tuple-element.184, s32[]{:T(128)S(6)} %select_n.19, bf16[12,256,256]{2,1,0:T(8,128)(2,1)} %get-tuple-element.186, s32[]{:T(128)S(6)} %select_n.18, ...), kind=kOutput, calls=%fused_computation.clone.1 | convolution fusion | flops 1075838976 | bytes 10749440 | tf_op jit(solution)/shard_map/while/body/rik,lk->ril/dot_general | solution.py:36
  68.2 0.6 dynamic_slice.47
  69.9 6.2 %convolution_add_fusion.2 = f32[16,256,256]{2,1,0:T(8,128)} fusion(f32[16,256,256]{2,1,0:T(8,128)} %get-tuple-element.169, bf16[3,16,256,256]{3,2,1,0:T(8,128)(2,1)} %get-tuple-element.184, s32[]{:T(128)S(6)} %select_n.19, bf16[12,256,256]{2,1,0:T(8,128)(2,1)} %get-tuple-element.186, s32[]{:T(128)S(6)} %select_n.18, ...), kind=kOutput, calls=%fused_computation.clone.1 | convolution fusion | flops 1075838976 | bytes 10749440 | tf_op jit(solution)/shard_map/while/body/rik,lk->ril/dot_general | solution.py:36
  78.5 6.2 %convolution_add_fusion.2 = f32[16,256,256]{2,1,0:T(8,128)} fusion(f32[16,256,256]{2,1,0:T(8,128)} %get-tuple-element.169, bf16[3,16,256,256]{3,2,1,0:T(8,128)(2,1)} %get-tuple-element.184, s32[]{:T(128)S(6)} %select_n.19, bf16[12,256,256]{2,1,0:T(8,128)(2,1)} %get-tuple-element.186, s32[]{:T(128)S(6)} %select_n.18, ...), kind=kOutput, calls=%fused_computation.clone.1 | convolution fusion | flops 1075838976 | bytes 10749440 | tf_op jit(solution)/shard_map/while/body/rik,lk->ril/dot_general | solution.py:36
  87.1 6.2 %convolution_add_fusion.2 = f32[16,256,256]{2,1,0:T(8,128)} fusion(f32[16,256,256]{2,1,0:T(8,128)} %get-tuple-element.169, bf16[3,16,256,256]{3,2,1,0:T(8,128)(2,1)} %get-tuple-element.184, s32[]{:T(128)S(6)} %select_n.19, bf16[12,256,256]{2,1,0:T(8,128)(2,1)} %get-tuple-element.186, s32[]{:T(128)S(6)} %select_n.18, ...), kind=kOutput, calls=%fused_computation.clone.1 | convolution fusion | flops 1075838976 | bytes 10749440 | tf_op jit(solution)/shard_map/while/body/rik,lk->ril/dot_general | solution.py:36
  95.6 6.2 %convolution_add_fusion.2 = f32[16,256,256]{2,1,0:T(8,128)} fusion(f32[16,256,256]{2,1,0:T(8,128)} %get-tuple-element.169, bf16[3,16,256,256]{3,2,1,0:T(8,128)(2,1)} %get-tuple-element.184, s32[]{:T(128)S(6)} %select_n.19, bf16[12,256,256]{2,1,0:T(8,128)(2,1)} %get-tuple-element.186, s32[]{:T(128)S(6)} %select_n.18, ...), kind=kOutput, calls=%fused_computation.clone.1 | convolution fusion | flops 1075838976 | bytes 10749440 | tf_op jit(solution)/shard_map/while/body/rik,lk->ril/dot_general | solution.py:36
  104.2 6.2 %convolution_add_fusion.2 = f32[16,256,256]{2,1,0:T(8,128)} fusion(f32[16,256,256]{2,1,0:T(8,128)} %get-tuple-element.169, bf16[3,16,256,256]{3,2,1,0:T(8,128)(2,1)} %get-tuple-element.184, s32[]{:T(128)S(6)} %select_n.19, bf16[12,256,256]{2,1,0:T(8,128)(2,1)} %get-tuple-element.186, s32[]{:T(128)S(6)} %select_n.18, ...), kind=kOutput, calls=%fused_computation.clone.1 | convolution fusion | flops 1075838976 | bytes 10749440 | tf_op jit(solution)/shard_map/while/body/rik,lk->ril/dot_general | solution.py:36
  112.8 6.2 %convolution_add_fusion.2 = f32[16,256,256]{2,1,0:T(8,128)} fusion(f32[16,256,256]{2,1,0:T(8,128)} %get-tuple-element.169, bf16[3,16,256,256]{3,2,1,0:T(8,128)(2,1)} %get-tuple-element.184, s32[]{:T(128)S(6)} %select_n.19, bf16[12,256,256]{2,1,0:T(8,128)(2,1)} %get-tuple-element.186, s32[]{:T(128)S(6)} %select_n.18, ...), kind=kOutput, calls=%fused_computation.clone.1 | convolution fusion | flops 1075838976 | bytes 10749440 | tf_op jit(solution)/shard_map/while/body/rik,lk->ril/dot_general | solution.py:36
  119.6 0.6 dynamic_slice.47
  121.3 6.2 %convolution_add_fusion.2 = f32[16,256,256]{2,1,0:T(8,128)} fusion(f32[16,256,256]{2,1,0:T(8,128)} %get-tuple-element.169, bf16[3,16,256,256]{3,2,1,0:T(8,128)(2,1)} %get-tuple-element.184, s32[]{:T(128)S(6)} %select_n.19, bf16[12,256,256]{2,1,0:T(8,128)(2,1)} %get-tuple-element.186, s32[]{:T(128)S(6)} %select_n.18, ...), kind=kOutput, calls=%fused_computation.clone.1 | convolution fusion | flops 1075838976 | bytes 10749440 | tf_op jit(solution)/shard_map/while/body/rik,lk->ril/dot_general | solution.py:36
  129.9 6.2 %convolution_add_fusion.2 = f32[16,256,256]{2,1,0:T(8,128)} fusion(f32[16,256,256]{2,1,0:T(8,128)} %get-tuple-element.169, bf16[3,16,256,256]{3,2,1,0:T(8,128)(2,1)} %get-tuple-element.184, s32[]{:T(128)S(6)} %select_n.19, bf16[12,256,256]{2,1,0:T(8,128)(2,1)} %get-tuple-element.186, s32[]{:T(128)S(6)} %select_n.18, ...), kind=kOutput, calls=%fused_computation.clone.1 | convolution fusion | flops 1075838976 | bytes 10749440 | tf_op jit(solution)/shard_map/while/body/rik,lk->ril/dot_general | solution.py:36
  138.5 6.2 %convolution_add_fusion.2 = f32[16,256,256]{2,1,0:T(8,128)} fusion(f32[16,256,256]{2,1,0:T(8,128)} %get-tuple-element.169, bf16[3,16,256,256]{3,2,1,0:T(8,128)(2,1)} %get-tuple-element.184, s32[]{:T(128)S(6)} %select_n.19, bf16[12,256,256]{2,1,0:T(8,128)(2,1)} %get-tuple-element.186, s32[]{:T(128)S(6)} %select_n.18, ...), kind=kOutput, calls=%fused_computation.clone.1 | convolution fusion | flops 1075838976 | bytes 10749440 | tf_op jit(solution)/shard_map/while/body/rik,lk->ril/dot_general | solution.py:36
  145.3 0.6 dynamic_slice.47
  147.1 6.2 %convolution_add_fusion.2 = f32[16,256,256]{2,1,0:T(8,128)} fusion(f32[16,256,256]{2,1,0:T(8,128)} %get-tuple-element.169, bf16[3,16,256,256]{3,2,1,0:T(8,128)(2,1)} %get-tuple-element.184, s32[]{:T(128)S(6)} %select_n.19, bf16[12,256,256]{2,1,0:T(8,128)(2,1)} %get-tuple-element.186, s32[]{:T(128)S(6)} %select_n.18, ...), kind=kOutput, calls=%fused_computation.clone.1 | convolution fusion | flops 1075838976 | bytes 10749440 | tf_op jit(solution)/shard_map/while/body/rik,lk->ril/dot_general | solution.py:36
  155.6 6.2 %convolution_add_fusion.2 = f32[16,256,256]{2,1,0:T(8,128)} fusion(f32[16,256,256]{2,1,0:T(8,128)} %get-tuple-element.169, bf16[3,16,256,256]{3,2,1,0:T(8,128)(2,1)} %get-tuple-element.184, s32[]{:T(128)S(6)} %select_n.19, bf16[12,256,256]{2,1,0:T(8,128)(2,1)} %get-tuple-element.186, s32[]{:T(128)S(6)} %select_n.18, ...), kind=kOutput, calls=%fused_computation.clone.1 | convolution fusion | flops 1075838976 | bytes 10749440 | tf_op jit(solution)/shard_map/while/body/rik,lk->ril/dot_general | solution.py:36
  162.5 3.8 %convert_bitcast_fusion = bf16[1,16,256,256]{3,2,1,0:T(8,128)(2,1)} fusion(f32[16,256,256]{2,1,0:T(8,128)} %get-tuple-element.97), kind=kLoop, calls=%fused_computation.12 | loop fusion | flops 1048576 | bytes 6291456 | tf_op jit(solution)/shard_map/broadcast_in_dim | solution.py:48
  (10 shorter events, 4.7 us)
Async XLA Ops:
  0.0 49.4 %collective-permute-start = (bf16[1,16,256,256]{3,2,1,0:T(8,128)(2,1)}, bf16[1,16,256,256]{3,2,1,0:T(8,128)(2,1)S(1)}, u32[]{:S(2)}, u32[]{:S(2)}) collective-permute-start(bf16[1,16,256,256]{3,2,1,0:T(8,128)(2,1)} %param.7), channel_id=1, source_target_pairs={{0,1},{1,2},{2,3},{3,4},{4,5},{5,6},{6,7},{7,8},{8,9},{9,10},{10,1... | collective-permute-start | bytes 6291464 | tf_op jit(solution)/shard_map/ppermute | solution.py:15
  3.7 47.3 %collective-permute-start.1 = (bf16[1,16,256,256]{3,2,1,0:T(8,128)(2,1)}, bf16[1,16,256,256]{3,2,1,0:T(8,128)(2,1)}, u32[]{:S(2)}, u32[]{:S(2)}) collective-permute-start(bf16[1,16,256,256]{3,2,1,0:T(8,128)(2,1)} %param.7), channel_id=1, source_target_pairs={{1,0},{2,1},{3,2},{4,3},{5,4},{6,5},{7,6},{8,7},{9,8},{10,9},{11,1... | collective-permute-start | bytes 6291464 | tf_op jit(solution)/shard_map/ppermute | solution.py:17
  56.5 2.5 %copy-start = (s32[12]{0:T(128)S(1)}, s32[12]{0:T(128)}, u32[]{:S(2)}) copy-start(s32[12]{0:T(128)} %param.10) | copy-start | bytes 148
where the time goes:
time: 167 us; the launch traced here: 166 us
  matrix products  74.3 us (44%)
  waiting for transfers between devices  45.4 us (27%)
  loops' own time  22.2 us (13%)
  local copies, waits for them, and re-layouts  9.44 us (6%)
  other arithmetic  9.27 us (6%)
  starting transfers between devices  5.62 us (3%)
    dot_general x12, matrix products, add_pair(): jnp.einsum('rik,lk->ril', mixed, right_op, preferred_element_type=jnp.flo...  74.3 us
    ppermute x1, waiting for transfers between devices, extended(): lax.ppermute(tail, axis, [(i, (i + 1) % count) for i in range(ends)])  43.8 us
    another operation x1, loops' own time, apply_pairs(): return lax.fori_loop(jnp.int32(0), last_slot, add_pair, empty)  22.2 us
    dynamic_slice x12, local copies, waits for them, and re-layouts, add_pair(): where_from = deltas[slot_index] + offset  6.99 us
    concatenate x1, other arithmetic, extended(): jnp.concatenate([lax.ppermute(tail, axis, [(i, (i + 1) % count) for i in...  5.5 us
    broadcast_in_dim x1, other arithmetic, on_device(): return running.astype(jnp.bfloat16)[None]  3.77 us
    ppermute x1, starting transfers between devices, extended(): lax.ppermute(tail, axis, [(i, (i + 1) % count) for i in range(ends)])  3.7 us
  transfers between devices with their start and end apart: 2, of which 2 were waited for; matrix products, arithmetic and copies ran while one was open for 0% of the time, Pallas kernels for 0%

commit v1 on v0

v1 whole, which is shorter than its diff:
```python
import functools

import jax
import jax.numpy as jnp
from jax import lax
from jax.experimental import pallas as pl
from jax.experimental.pallas import tpu as pltpu
from jax.sharding import PartitionSpec as P

CHUNKS = 4


def neighbours(block, axis):
    count = lax.axis_size(axis)
    from_prev = lax.ppermute(block, axis, [(i, i + 1) for i in range(count - 1)])
    from_next = lax.ppermute(block, axis, [(i + 1, i) for i in range(count - 1)])
    return from_prev, from_next


def pair_kernel(deltas_ref, count_ref, prev_ref, own_ref, next_ref, left_ref, right_ref, out_ref, acc_ref):
    k = pl.program_id(0)

    @pl.when(k == 0)
    def _():
        acc_ref[...] = jnp.zeros_like(acc_ref)

    @pl.when(k < count_ref[0])
    def _():
        delta = deltas_ref[k]
        left = left_ref[0]
        right = right_ref[0]

        def run(src_ref):
            def body(r, carry):
                mixed = jnp.dot(left, src_ref[r], preferred_element_type=jnp.float32).astype(jnp.bfloat16)
                acc_ref[r] += lax.dot_general(
                    mixed, right, (((1,), (1,)), ((), ())), preferred_element_type=jnp.float32
                )
                return carry

            lax.fori_loop(0, src_ref.shape[0], body, 0)

        for d, ref in ((-1, prev_ref), (0, own_ref), (1, next_ref)):
            pl.when(delta == d)(functools.partial(run, ref))

    @pl.when(k == pl.num_programs(0) - 1)
    def _():
        out_ref[...] = acc_ref[...].astype(out_ref.dtype)


def apply_pairs(prev, own, nxt, left_ops, right_ops, deltas, count):
    rows, width = own.shape[0], own.shape[1]
    slots = left_ops.shape[0]
    whole = pl.BlockSpec((rows, width, width), lambda k, d, c: (0, 0, 0))
    per_slot = pl.BlockSpec((1, width, width), lambda k, d, c: (jnp.minimum(k, c[0] - 1), 0, 0))
    flops = 4 * slots * rows * width ** 3
    moved = 2 * (3 * rows * width * width + 2 * slots * width * width + rows * width * width)
    return pl.pallas_call(
        pair_kernel,
        out_shape=jax.ShapeDtypeStruct((rows, width, width), jnp.bfloat16),
        grid_spec=pltpu.PrefetchScalarGridSpec(
            num_scalar_prefetch=2,
            grid=(slots,),
            in_specs=[whole, whole, whole, per_slot, per_slot],
            out_specs=whole,
            scratch_shapes=[pltpu.VMEM((rows, width, width), jnp.float32)],
        ),
        cost_estimate=pl.CostEstimate(flops=flops, bytes_accessed=moved, transcendentals=0),
    )(deltas, count, prev, own, nxt, left_ops, right_ops)


def on_device(wave, left_ops, right_ops, deltas, counts):
    own = wave[0]
    roots = own.shape[0]
    step = roots // CHUNKS
    outs = []
    for j in range(CHUNKS):
        part = own[j * step:(j + 1) * step]
        prev, nxt = neighbours(part, "sector")
        outs.append(apply_pairs(prev, part, nxt, left_ops, right_ops, deltas, counts))
    return jnp.concatenate(outs, 0)[None]


def solution(mesh):
    return jax.shard_map(
        on_device,
        mesh=mesh,
        in_specs=(
            P(("group", "sector"), None, None, None),
            P(("group", "sector"), None, None),
            P(("group", "sector"), None, None),
            P(("group", "sector")),
            P(("group", "sector")),
        ),
        out_specs=P(("group", "sector"), None, None, None),
        check_vma=False,
    )
```

time: 167 us -> 121 us (0.72)
  the two profiles are of different devices: /device:TPU:17 before, /device:TPU:11 now
where the time goes in v1:
time: 121 us; the launch traced here: 120 us
  Pallas kernels  80.4 us (66%)
  starting transfers between devices  21.9 us (18%)
  waiting for transfers between devices  11.3 us (9%)
  local copies, waits for them, and re-layouts  3.28 us (3%)
  other arithmetic  2.62 us (2%)
    pallas_call x4, Pallas kernels, apply_pairs(): pl.pallas_call(pair_kernel, out_shape=jax.ShapeDtypeStruct((rows, width,...  80.4 us
    ppermute x4, starting transfers between devices, neighbours(): lax.ppermute(block, axis, [(i, i + 1) for i in range(count - 1)])  13 us
    ppermute x4, starting transfers between devices, neighbours(): lax.ppermute(block, axis, [(i + 1, i) for i in range(count - 1)])  8.94 us
    ppermute x4, waiting for transfers between devices, neighbours(): lax.ppermute(block, axis, [(i + 1, i) for i in range(count - 1)])  7.4 us
    ppermute x4, waiting for transfers between devices, neighbours(): lax.ppermute(block, axis, [(i, i + 1) for i in range(count - 1)])  3.87 us
    broadcast_in_dim x1, other arithmetic, on_device(): return jnp.concatenate(outs, 0)[None]  2.62 us
  transfers between devices with their start and end apart: 8, of which 2 were waited for; matrix products, arithmetic and copies ran while one was open for 0% of the time, Pallas kernels for 50%

profile of v1, /device:TPU:11, one launch (start us, length us, event | category | flops | bytes accessed | tf_op | source)
XLA Modules:
  0.0 120.3 jit_solution(8105174154935164485)
XLA Ops:
  0.0 1.7 %slice_bitcast_fusion.3 = (bf16[4,256,256]{2,1,0:T(8,128)(2,1)S(1)}, bf16[4,256,256]{2,1,0:T(8,128)(2,1)S(1)}, bf16[4,256,256]{2,1,0:T(8,128)(2,1)S(1)}, bf16[4,256,256]{2,1,0:T(8,128)(2,1)S(1)}) fusion(bf16[1,16,256,256]{3,2,1,0:T(8,128)(2,1)} %param.5), kind=kLoop, calls=%fused_computation.4 | loop fusion | bytes 4194304 | tf_op jit(solution)/shard_map/slice | solution.py:78
  1.7 0.0 copy-start.1
  1.7 2.6 %collective-permute-start.1 = (bf16[4,256,256]{2,1,0:T(8,128)(2,1)S(1)}, bf16[4,256,256]{2,1,0:T(8,128)(2,1)S(1)}, u32[]{:S(2)}, u32[]{:S(2)}) collective-permute-start(bf16[4,256,256]{2,1,0:T(8,128)(2,1)S(1)} %get-tuple-element.5.own_ref), channel_id=1, source_target_pairs={{1,0},{2,1},{3,2},{4,3},{5,4},{6,5},{7,6},{8,7},{9,8},{10,9},{11,1... | collective-permute-start | bytes 1572872 | tf_op jit(solution)/shard_map/ppermute | solution.py:16
  4.3 3.0 %collective-permute-start = (bf16[4,256,256]{2,1,0:T(8,128)(2,1)S(1)}, bf16[4,256,256]{2,1,0:T(8,128)(2,1)S(1)}, u32[]{:S(2)}, u32[]{:S(2)}) collective-permute-start(bf16[4,256,256]{2,1,0:T(8,128)(2,1)S(1)} %get-tuple-element.5.own_ref), channel_id=1, source_target_pairs={{0,1},{1,2},{2,3},{3,4},{4,5},{5,6},{6,7},{7,8},{8,9},{9,10},{10,1... | collective-permute-start | bytes 1572872 | tf_op jit(solution)/shard_map/ppermute | solution.py:15
  7.4 1.9 %collective-permute-start.3 = (bf16[4,256,256]{2,1,0:T(8,128)(2,1)S(1)}, bf16[4,256,256]{2,1,0:T(8,128)(2,1)S(1)}, u32[]{:S(2)}, u32[]{:S(2)}) collective-permute-start(bf16[4,256,256]{2,1,0:T(8,128)(2,1)S(1)} %get-tuple-element.6.own_ref), channel_id=1, source_target_pairs={{1,0},{2,1},{3,2},{4,3},{5,4},{6,5},{7,6},{8,7},{9,8},{10,9},{11,1... | collective-permute-start | bytes 1572872 | tf_op jit(solution)/shard_map/ppermute | solution.py:16
  9.3 3.6 %collective-permute-start.2 = (bf16[4,256,256]{2,1,0:T(8,128)(2,1)S(1)}, bf16[4,256,256]{2,1,0:T(8,128)(2,1)}, u32[]{:S(2)}, u32[]{:S(2)}) collective-permute-start(bf16[4,256,256]{2,1,0:T(8,128)(2,1)S(1)} %get-tuple-element.6.own_ref), channel_id=1, source_target_pairs={{0,1},{1,2},{2,3},{3,4},{4,5},{5,6},{6,7},{7,8},{8,9},{9,10},{10,1... | collective-permute-start | bytes 1572872 | tf_op jit(solution)/shard_map/ppermute | solution.py:15
  12.9 2.5 %collective-permute-start.7 = (bf16[4,256,256]{2,1,0:T(8,128)(2,1)S(1)}, bf16[4,256,256]{2,1,0:T(8,128)(2,1)S(1)}, u32[]{:S(2)}, u32[]{:S(2)}) collective-permute-start(bf16[4,256,256]{2,1,0:T(8,128)(2,1)S(1)} %get-tuple-element.7.own_ref), channel_id=1, source_target_pairs={{1,0},{2,1},{3,2},{4,3},{5,4},{6,5},{7,6},{8,7},{9,8},{10,9},{11,1... | collective-permute-start | bytes 1572872 | tf_op jit(solution)/shard_map/ppermute | solution.py:16
  16.1 7.4 %collective-permute-done.1.next_ref = bf16[4,256,256]{2,1,0:T(8,128)(2,1)S(1)} collective-permute-done((bf16[4,256,256]{2,1,0:T(8,128)(2,1)S(1)}, bf16[4,256,256]{2,1,0:T(8,128)(2,1)S(1)}, u32[]{:S(2)}, u32[]{:S(2)}) %collective-permute-start.1) | collective-permute-done | bytes 524320 | tf_op jit(solution)/shard_map/ppermute | solution.py:16
  23.5 1.9 %collective-permute-start.6 = (bf16[4,256,256]{2,1,0:T(8,128)(2,1)S(1)}, bf16[4,256,256]{2,1,0:T(8,128)(2,1)}, u32[]{:S(2)}, u32[]{:S(2)}) collective-permute-start(bf16[4,256,256]{2,1,0:T(8,128)(2,1)S(1)} %get-tuple-element.7.own_ref), channel_id=1, source_target_pairs={{0,1},{1,2},{2,3},{3,4},{4,5},{5,6},{6,7},{7,8},{8,9},{9,10},{10,1... | collective-permute-start | bytes 1572872 | tf_op jit(solution)/shard_map/ppermute | solution.py:15
  25.4 3.9 %collective-permute-done.prev_ref = bf16[4,256,256]{2,1,0:T(8,128)(2,1)S(1)} collective-permute-done((bf16[4,256,256]{2,1,0:T(8,128)(2,1)S(1)}, bf16[4,256,256]{2,1,0:T(8,128)(2,1)S(1)}, u32[]{:S(2)}, u32[]{:S(2)}) %collective-permute-start) | collective-permute-done | bytes 524320 | tf_op jit(solution)/shard_map/ppermute | solution.py:15
  29.3 0.8 copy-done.10
  30.1 1.9 %collective-permute-start.5 = (bf16[4,256,256]{2,1,0:T(8,128)(2,1)S(1)}, bf16[4,256,256]{2,1,0:T(8,128)(2,1)}, u32[]{:S(2)}, u32[]{:S(2)}) collective-permute-start(bf16[4,256,256]{2,1,0:T(8,128)(2,1)S(1)} %get-tuple-element.8.own_ref), channel_id=1, source_target_pairs={{1,0},{2,1},{3,2},{4,3},{5,4},{6,5},{7,6},{8,7},{9,8},{10,9},{11,1... | collective-permute-start | bytes 1572872 | tf_op jit(solution)/shard_map/ppermute | solution.py:16
  32.0 20.1 %shard_map.55 = bf16[4,256,256]{2,1,0:T(8,128)(2,1)} custom-call(s32[12]{0:T(128)} %deltas_ref.7, s32[1]{0:T(128)S(6)} %copy.6.count_ref, bf16[4,256,256]{2,1,0:T(8,128)(2,1)} %copy-done.10, bf16[4,256,256]{2,1,0:T(8,128)(2,1)} %copy-done.3, bf16[4,256,256]{2,1,0:T(8,128)(2,1)} %copy-done.9, bf16[12,256,256]{2,1,0:T(8,128)(2,1)} %left_ref.7, ...), custom_call_target="tpu_custom_call" | custom-call | flops 3221225472 | bytes 5242880 | tf_op jit(solution)/shard_map/pallas_call | solution.py:58
  52.1 0.0 collective-permute-done.3.next_ref
  52.1 4.4 %collective-permute-start.4 = (bf16[4,256,256]{2,1,0:T(8,128)(2,1)S(1)}, bf16[4,256,256]{2,1,0:T(8,128)(2,1)}, u32[]{:S(2)}, u32[]{:S(2)}) collective-permute-start(bf16[4,256,256]{2,1,0:T(8,128)(2,1)S(1)} %get-tuple-element.8.own_ref), channel_id=1, source_target_pairs={{0,1},{1,2},{2,3},{3,4},{4,5},{5,6},{6,7},{7,8},{8,9},{9,10},{10,1... | collective-permute-start | bytes 1572872 | tf_op jit(solution)/shard_map/ppermute | solution.py:15
  56.5 0.0 collective-permute-done.2.prev_ref
  56.5 20.0 %shard_map.56 = bf16[4,256,256]{2,1,0:T(8,128)(2,1)} custom-call(s32[12]{0:T(128)} %deltas_ref.7, s32[1]{0:T(128)S(6)} %copy.6.count_ref, bf16[4,256,256]{2,1,0:T(8,128)(2,1)} %collective-permute-done.2.prev_ref, bf16[4,256,256]{2,1,0:T(8,128)(2,1)} %copy-done.2, bf16[4,256,256]{2,1,0:T(8,128)(2,1)} %copy-done.8, bf16[12,256,256]{2,1,0:T(8,128)(2,1)} %left_ref.7, ...), custom_call_target="tpu_custom_call" | custom-call | flops 3221225472 | bytes 5242880 | tf_op jit(solution)/shard_map/pallas_call | solution.py:58
  76.6 0.0 collective-permute-done.7.next_ref
  76.6 0.0 collective-permute-done.6.prev_ref
  76.6 0.8 copy-done.7
  77.4 20.0 %shard_map.58 = bf16[4,256,256]{2,1,0:T(8,128)(2,1)} custom-call(s32[12]{0:T(128)} %deltas_ref.7, s32[1]{0:T(128)S(6)} %copy.6.count_ref, bf16[4,256,256]{2,1,0:T(8,128)(2,1)} %collective-permute-done.6.prev_ref, bf16[4,256,256]{2,1,0:T(8,128)(2,1)} %copy-done.1, bf16[4,256,256]{2,1,0:T(8,128)(2,1)} %copy-done.7, bf16[12,256,256]{2,1,0:T(8,128)(2,1)} %left_ref.7, ...), custom_call_target="tpu_custom_call" | custom-call | flops 3221225472 | bytes 5242880 | tf_op jit(solution)/shard_map/pallas_call | solution.py:58
  97.4 0.0 collective-permute-done.4.prev_ref
  97.4 20.2 %shard_map.57 = bf16[4,256,256]{2,1,0:T(8,128)(2,1)} custom-call(s32[12]{0:T(128)} %deltas_ref.7, s32[1]{0:T(128)S(6)} %copy.6.count_ref, bf16[4,256,256]{2,1,0:T(8,128)(2,1)} %collective-permute-done.4.prev_ref, bf16[4,256,256]{2,1,0:T(8,128)(2,1)} %copy-done, bf16[4,256,256]{2,1,0:T(8,128)(2,1)} %collective-permute-done.5.next_ref, ...), custom_call_target="tpu_custom_call" | custom-call | flops 3221225472 | bytes 5242880 | tf_op jit(solution)/shard_map/pallas_call | solution.py:58
  117.7 2.6 %maximum_bitcast_fusion = bf16[1,16,256,256]{3,2,1,0:T(8,128)(2,1)} fusion(bf16[4,256,256]{2,1,0:T(8,128)(2,1)S(1)} %copy-done.6, bf16[4,256,256]{2,1,0:T(8,128)(2,1)} %shard_map.57, bf16[4,256,256]{2,1,0:T(8,128)(2,1)S(1)} %copy-done.5, bf16[4,256,256]{2,1,0:T(8,128)(2,1)S(1)} %copy-done.4), kind=kLoop, calls=%fused_computation | loop fusion | flops 3145728 | bytes 4194304 | tf_op jit(solution)/shard_map/broadcast_in_dim | solution.py:81
  (20 shorter events, 0.0 us)
Async XLA Ops:
  1.7 30.3 %copy-start.3 = (bf16[4,256,256]{2,1,0:T(8,128)(2,1)}, bf16[4,256,256]{2,1,0:T(8,128)(2,1)S(1)}, u32[]{:S(2)}) copy-start(bf16[4,256,256]{2,1,0:T(8,128)(2,1)S(1)} %get-tuple-element.5.own_ref) | copy-start | bytes 1572868
  1.7 50.4 %copy-start.1 = (bf16[4,256,256]{2,1,0:T(8,128)(2,1)}, bf16[4,256,256]{2,1,0:T(8,128)(2,1)S(1)}, u32[]{:S(2)}) copy-start(bf16[4,256,256]{2,1,0:T(8,128)(2,1)S(1)} %get-tuple-element.7.own_ref) | copy-start | bytes 1572868
  1.7 50.4 %copy-start.2 = (bf16[4,256,256]{2,1,0:T(8,128)(2,1)}, bf16[4,256,256]{2,1,0:T(8,128)(2,1)S(1)}, u32[]{:S(2)}) copy-start(bf16[4,256,256]{2,1,0:T(8,128)(2,1)S(1)} %get-tuple-element.6.own_ref) | copy-start | bytes 1572868
  1.7 50.4 %copy-start = (bf16[4,256,256]{2,1,0:T(8,128)(2,1)}, bf16[4,256,256]{2,1,0:T(8,128)(2,1)S(1)}, u32[]{:S(2)}) copy-start(bf16[4,256,256]{2,1,0:T(8,128)(2,1)S(1)} %get-tuple-element.8.own_ref) | copy-start | bytes 1572868
  1.7 21.8 %collective-permute-start.1 = (bf16[4,256,256]{2,1,0:T(8,128)(2,1)S(1)}, bf16[4,256,256]{2,1,0:T(8,128)(2,1)S(1)}, u32[]{:S(2)}, u32[]{:S(2)}) collective-permute-start(bf16[4,256,256]{2,1,0:T(8,128)(2,1)S(1)} %get-tuple-element.5.own_ref), channel_id=1, source_target_pairs={{1,0},{2,1},{3,2},{4,3},{5,4},{6,5},{7,6},{8,7},{9,8},{10,9},{11,1... | collective-permute-start | bytes 1572872 | tf_op jit(solution)/shard_map/ppermute | solution.py:16
  4.3 25.0 %collective-permute-start = (bf16[4,256,256]{2,1,0:T(8,128)(2,1)S(1)}, bf16[4,256,256]{2,1,0:T(8,128)(2,1)S(1)}, u32[]{:S(2)}, u32[]{:S(2)}) collective-permute-start(bf16[4,256,256]{2,1,0:T(8,128)(2,1)S(1)} %get-tuple-element.5.own_ref), channel_id=1, source_target_pairs={{0,1},{1,2},{2,3},{3,4},{4,5},{5,6},{6,7},{7,8},{8,9},{9,10},{10,1... | collective-permute-start | bytes 1572872 | tf_op jit(solution)/shard_map/ppermute | solution.py:15
  7.4 44.7 %collective-permute-start.3 = (bf16[4,256,256]{2,1,0:T(8,128)(2,1)S(1)}, bf16[4,256,256]{2,1,0:T(8,128)(2,1)S(1)}, u32[]{:S(2)}, u32[]{:S(2)}) collective-permute-start(bf16[4,256,256]{2,1,0:T(8,128)(2,1)S(1)} %get-tuple-element.6.own_ref), channel_id=1, source_target_pairs={{1,0},{2,1},{3,2},{4,3},{5,4},{6,5},{7,6},{8,7},{9,8},{10,9},{11,1... | collective-permute-start | bytes 1572872 | tf_op jit(solution)/shard_map/ppermute | solution.py:16
  9.3 47.2 %collective-permute-start.2 = (bf16[4,256,256]{2,1,0:T(8,128)(2,1)S(1)}, bf16[4,256,256]{2,1,0:T(8,128)(2,1)}, u32[]{:S(2)}, u32[]{:S(2)}) collective-permute-start(bf16[4,256,256]{2,1,0:T(8,128)(2,1)S(1)} %get-tuple-element.6.own_ref), channel_id=1, source_target_pairs={{0,1},{1,2},{2,3},{3,4},{4,5},{5,6},{6,7},{7,8},{8,9},{9,10},{10,1... | collective-permute-start | bytes 1572872 | tf_op jit(solution)/shard_map/ppermute | solution.py:15
  12.9 63.6 %collective-permute-start.7 = (bf16[4,256,256]{2,1,0:T(8,128)(2,1)S(1)}, bf16[4,256,256]{2,1,0:T(8,128)(2,1)S(1)}, u32[]{:S(2)}, u32[]{:S(2)}) collective-permute-start(bf16[4,256,256]{2,1,0:T(8,128)(2,1)S(1)} %get-tuple-element.7.own_ref), channel_id=1, source_target_pairs={{1,0},{2,1},{3,2},{4,3},{5,4},{6,5},{7,6},{8,7},{9,8},{10,9},{11,1... | collective-permute-start | bytes 1572872 | tf_op jit(solution)/shard_map/ppermute | solution.py:16
  23.5 5.8 %copy-start.9 = (bf16[4,256,256]{2,1,0:T(8,128)(2,1)}, bf16[4,256,256]{2,1,0:T(8,128)(2,1)S(1)}, u32[]{:S(2)}) copy-start(bf16[4,256,256]{2,1,0:T(8,128)(2,1)S(1)} %collective-permute-done.1.next_ref) | copy-start | bytes 1572868
  23.5 53.1 %collective-permute-start.6 = (bf16[4,256,256]{2,1,0:T(8,128)(2,1)S(1)}, bf16[4,256,256]{2,1,0:T(8,128)(2,1)}, u32[]{:S(2)}, u32[]{:S(2)}) collective-permute-start(bf16[4,256,256]{2,1,0:T(8,128)(2,1)S(1)} %get-tuple-element.7.own_ref), channel_id=1, source_target_pairs={{0,1},{1,2},{2,3},{3,4},{4,5},{5,6},{6,7},{7,8},{8,9},{9,10},{10,1... | collective-permute-start | bytes 1572872 | tf_op jit(solution)/shard_map/ppermute | solution.py:15
  29.3 0.8 copy-start.10
  30.1 67.3 %collective-permute-start.5 = (bf16[4,256,256]{2,1,0:T(8,128)(2,1)S(1)}, bf16[4,256,256]{2,1,0:T(8,128)(2,1)}, u32[]{:S(2)}, u32[]{:S(2)}) collective-permute-start(bf16[4,256,256]{2,1,0:T(8,128)(2,1)S(1)} %get-tuple-element.8.own_ref), channel_id=1, source_target_pairs={{1,0},{2,1},{3,2},{4,3},{5,4},{6,5},{7,6},{8,7},{9,8},{10,9},{11,1... | collective-permute-start | bytes 1572872 | tf_op jit(solution)/shard_map/ppermute | solution.py:16
  52.1 4.4 %copy-start.8 = (bf16[4,256,256]{2,1,0:T(8,128)(2,1)}, bf16[4,256,256]{2,1,0:T(8,128)(2,1)S(1)}, u32[]{:S(2)}) copy-start(bf16[4,256,256]{2,1,0:T(8,128)(2,1)S(1)} %collective-permute-done.3.next_ref) | copy-start | bytes 1572868
  52.1 45.3 %collective-permute-start.4 = (bf16[4,256,256]{2,1,0:T(8,128)(2,1)S(1)}, bf16[4,256,256]{2,1,0:T(8,128)(2,1)}, u32[]{:S(2)}, u32[]{:S(2)}) collective-permute-start(bf16[4,256,256]{2,1,0:T(8,128)(2,1)S(1)} %get-tuple-element.8.own_ref), channel_id=1, source_target_pairs={{0,1},{1,2},{2,3},{3,4},{4,5},{5,6},{6,7},{7,8},{8,9},{9,10},{10,1... | collective-permute-start | bytes 1572872 | tf_op jit(solution)/shard_map/ppermute | solution.py:15
  76.6 0.8 copy-start.7
  97.4 20.3 %copy-start.4 = (bf16[4,256,256]{2,1,0:T(8,128)(2,1)S(1)}, bf16[4,256,256]{2,1,0:T(8,128)(2,1)}, u32[]{:S(2)}) copy-start(bf16[4,256,256]{2,1,0:T(8,128)(2,1)} %shard_map.55) | copy-start | bytes 1572868
  97.4 20.3 %copy-start.5 = (bf16[4,256,256]{2,1,0:T(8,128)(2,1)S(1)}, bf16[4,256,256]{2,1,0:T(8,128)(2,1)}, u32[]{:S(2)}) copy-start(bf16[4,256,256]{2,1,0:T(8,128)(2,1)} %shard_map.56) | copy-start | bytes 1572868
  97.4 20.3 %copy-start.6 = (bf16[4,256,256]{2,1,0:T(8,128)(2,1)S(1)}, bf16[4,256,256]{2,1,0:T(8,128)(2,1)}, u32[]{:S(2)}) copy-start(bf16[4,256,256]{2,1,0:T(8,128)(2,1)} %shard_map.58) | copy-start | bytes 1572868

commit v2 on v1

--- a/solution.py
+++ b/solution.py
@@ -17,8 +17,9 @@
     return from_prev, from_next
 
 
-def pair_kernel(deltas_ref, count_ref, prev_ref, own_ref, next_ref, left_ref, right_ref, out_ref, acc_ref):
+def pair_kernel(deltas_ref, count_ref, prev_ref, own_ref, next_ref, left_ref, right_ref, out_ref, acc_ref, mixed_ref):
     k = pl.program_id(0)
+    rows, width = own_ref.shape[0], own_ref.shape[1]
 
     @pl.when(k == 0)
     def _():
@@ -28,24 +29,23 @@
     def _():
         delta = deltas_ref[k]
         left = left_ref[0]
-        right = right_ref[0]
 
         def run(src_ref):
-            def body(r, carry):
-                mixed = jnp.dot(left, src_ref[r], preferred_element_type=jnp.float32).astype(jnp.bfloat16)
-                acc_ref[r] += lax.dot_general(
-                    mixed, right, (((1,), (1,)), ((), ())), preferred_element_type=jnp.float32
-                )
-                return carry
-
-            lax.fori_loop(0, src_ref.shape[0], body, 0)
+            for r in range(rows):
+                mixed_ref[pl.ds(r * width, width), :] = jnp.dot(
+                    left, src_ref[r], preferred_element_type=jnp.float32
+                ).astype(jnp.bfloat16)
 
         for d, ref in ((-1, prev_ref), (0, own_ref), (1, next_ref)):
             pl.when(delta == d)(functools.partial(run, ref))
+        acc_ref[...] += lax.dot_general(
+            mixed_ref[...], right_ref[0], (((1,), (1,)), ((), ())), preferred_element_type=jnp.float32
+        )
 
     @pl.when(k == pl.num_programs(0) - 1)
     def _():
-        out_ref[...] = acc_ref[...].astype(out_ref.dtype)
+        for r in range(rows):
+            out_ref[r] = acc_ref[pl.ds(r * width, width), :].astype(out_ref.dtype)
 
 
 def apply_pairs(prev, own, nxt, left_ops, right_ops, deltas, count):
@@ -63,7 +63,10 @@
             grid=(slots,),
             in_specs=[whole, whole, whole, per_slot, per_slot],
             out_specs=whole,
-            scratch_shapes=[pltpu.VMEM((rows, width, width), jnp.float32)],
+            scratch_shapes=[
+                pltpu.VMEM((rows * width, width), jnp.float32),
+                pltpu.VMEM((rows * width, width), jnp.bfloat16),
+            ],
         ),
         cost_estimate=pl.CostEstimate(flops=flops, bytes_accessed=moved, transcendentals=0),
     )(deltas, count, prev, own, nxt, left_ops, right_ops)

time: 121 us -> 91.7 us (0.76)
  the two profiles are of different devices: /device:TPU:11 before, /device:TPU:23 now
where the time goes in v2:
time: 91.7 us; the launch traced here: 89.9 us
  Pallas kernels  51.1 us (56%)
  starting transfers between devices  32 us (35%)
  local copies, waits for them, and re-layouts  3.27 us (4%)
  other arithmetic  2.62 us (3%)
    pallas_call x4, Pallas kernels, apply_pairs(): pl.pallas_call(pair_kernel, out_shape=jax.ShapeDtypeStruct((rows, width,...  51.1 us
    ppermute x4, starting transfers between devices, neighbours(): lax.ppermute(block, axis, [(i + 1, i) for i in range(count - 1)])  17.1 us
    ppermute x4, starting transfers between devices, neighbours(): lax.ppermute(block, axis, [(i, i + 1) for i in range(count - 1)])  14.9 us
    broadcast_in_dim x1, other arithmetic, on_device(): return jnp.concatenate(outs, 0)[None]  2.62 us
  transfers between devices with their start and end apart: 8, of which 0 were waited for; matrix products, arithmetic and copies ran while one was open for 0% of the time, Pallas kernels for 42%

profile of v2, /device:TPU:23, one launch (start us, length us, event | category | flops | bytes accessed | tf_op | source)
XLA Modules:
  0.0 89.9 jit_solution(2506109084850654337)
XLA Ops:
  0.0 1.7 %slice_bitcast_fusion.3 = (bf16[4,256,256]{2,1,0:T(8,128)(2,1)S(1)}, bf16[4,256,256]{2,1,0:T(8,128)(2,1)S(1)}, bf16[4,256,256]{2,1,0:T(8,128)(2,1)S(1)}, bf16[4,256,256]{2,1,0:T(8,128)(2,1)S(1)}) fusion(bf16[1,16,256,256]{3,2,1,0:T(8,128)(2,1)} %param.5), kind=kLoop, calls=%fused_computation.4 | loop fusion | bytes 4194304 | tf_op jit(solution)/shard_map/slice | solution.py:81
  1.7 0.0 copy-start.1
  1.7 2.6 %collective-permute-start.1 = (bf16[4,256,256]{2,1,0:T(8,128)(2,1)S(1)}, bf16[4,256,256]{2,1,0:T(8,128)(2,1)S(1)}, u32[]{:S(2)}, u32[]{:S(2)}) collective-permute-start(bf16[4,256,256]{2,1,0:T(8,128)(2,1)S(1)} %get-tuple-element.5.own_ref), channel_id=1, source_target_pairs={{1,0},{2,1},{3,2},{4,3},{5,4},{6,5},{7,6},{8,7},{9,8},{10,9},{11,1... | collective-permute-start | bytes 1572872 | tf_op jit(solution)/shard_map/ppermute | solution.py:16
  4.3 3.9 %collective-permute-start = (bf16[4,256,256]{2,1,0:T(8,128)(2,1)S(1)}, bf16[4,256,256]{2,1,0:T(8,128)(2,1)S(1)}, u32[]{:S(2)}, u32[]{:S(2)}) collective-permute-start(bf16[4,256,256]{2,1,0:T(8,128)(2,1)S(1)} %get-tuple-element.5.own_ref), channel_id=1, source_target_pairs={{0,1},{1,2},{2,3},{3,4},{4,5},{5,6},{6,7},{7,8},{8,9},{9,10},{10,1... | collective-permute-start | bytes 1572872 | tf_op jit(solution)/shard_map/ppermute | solution.py:15
  8.2 1.9 %collective-permute-start.3 = (bf16[4,256,256]{2,1,0:T(8,128)(2,1)S(1)}, bf16[4,256,256]{2,1,0:T(8,128)(2,1)S(1)}, u32[]{:S(2)}, u32[]{:S(2)}) collective-permute-start(bf16[4,256,256]{2,1,0:T(8,128)(2,1)S(1)} %get-tuple-element.6.own_ref), channel_id=1, source_target_pairs={{1,0},{2,1},{3,2},{4,3},{5,4},{6,5},{7,6},{8,7},{9,8},{10,9},{11,1... | collective-permute-start | bytes 1572872 | tf_op jit(solution)/shard_map/ppermute | solution.py:16
  10.1 4.5 %collective-permute-start.2 = (bf16[4,256,256]{2,1,0:T(8,128)(2,1)S(1)}, bf16[4,256,256]{2,1,0:T(8,128)(2,1)}, u32[]{:S(2)}, u32[]{:S(2)}) collective-permute-start(bf16[4,256,256]{2,1,0:T(8,128)(2,1)S(1)} %get-tuple-element.6.own_ref), channel_id=1, source_target_pairs={{0,1},{1,2},{2,3},{3,4},{4,5},{5,6},{6,7},{7,8},{8,9},{9,10},{10,1... | collective-permute-start | bytes 1572872 | tf_op jit(solution)/shard_map/ppermute | solution.py:15
  14.7 1.9 %collective-permute-start.7 = (bf16[4,256,256]{2,1,0:T(8,128)(2,1)S(1)}, bf16[4,256,256]{2,1,0:T(8,128)(2,1)S(1)}, u32[]{:S(2)}, u32[]{:S(2)}) collective-permute-start(bf16[4,256,256]{2,1,0:T(8,128)(2,1)S(1)} %get-tuple-element.7.own_ref), channel_id=1, source_target_pairs={{1,0},{2,1},{3,2},{4,3},{5,4},{6,5},{7,6},{8,7},{9,8},{10,9},{11,1... | collective-permute-start | bytes 1572872 | tf_op jit(solution)/shard_map/ppermute | solution.py:16
  17.3 0.0 collective-permute-done.1.next_ref
  17.3 4.5 %collective-permute-start.6 = (bf16[4,256,256]{2,1,0:T(8,128)(2,1)S(1)}, bf16[4,256,256]{2,1,0:T(8,128)(2,1)}, u32[]{:S(2)}, u32[]{:S(2)}) collective-permute-start(bf16[4,256,256]{2,1,0:T(8,128)(2,1)S(1)} %get-tuple-element.7.own_ref), channel_id=1, source_target_pairs={{0,1},{1,2},{2,3},{3,4},{4,5},{5,6},{6,7},{7,8},{8,9},{9,10},{10,1... | collective-permute-start | bytes 1572872 | tf_op jit(solution)/shard_map/ppermute | solution.py:15
  21.8 0.0 collective-permute-done.prev_ref
  21.9 0.8 copy-done.10
  22.6 10.7 %collective-permute-start.5 = (bf16[4,256,256]{2,1,0:T(8,128)(2,1)S(1)}, bf16[4,256,256]{2,1,0:T(8,128)(2,1)}, u32[]{:S(2)}, u32[]{:S(2)}) collective-permute-start(bf16[4,256,256]{2,1,0:T(8,128)(2,1)S(1)} %get-tuple-element.8.own_ref), channel_id=1, source_target_pairs={{1,0},{2,1},{3,2},{4,3},{5,4},{6,5},{7,6},{8,7},{9,8},{10,9},{11,1... | collective-permute-start | bytes 1572872 | tf_op jit(solution)/shard_map/ppermute | solution.py:16
  33.4 12.7 %shard_map.55 = bf16[4,256,256]{2,1,0:T(8,128)(2,1)} custom-call(s32[12]{0:T(128)} %deltas_ref.7, s32[1]{0:T(128)S(6)} %copy.6.count_ref, bf16[4,256,256]{2,1,0:T(8,128)(2,1)} %copy-done.10, bf16[4,256,256]{2,1,0:T(8,128)(2,1)} %copy-done.3, bf16[4,256,256]{2,1,0:T(8,128)(2,1)} %copy-done.9, bf16[12,256,256]{2,1,0:T(8,128)(2,1)} %left_ref.7, ...), custom_call_target="tpu_custom_call" | custom-call | flops 3221225472 | bytes 5242880 | tf_op jit(solution)/shard_map/pallas_call | solution.py:58
  46.1 0.0 collective-permute-done.3.next_ref
  46.1 1.9 %collective-permute-start.4 = (bf16[4,256,256]{2,1,0:T(8,128)(2,1)S(1)}, bf16[4,256,256]{2,1,0:T(8,128)(2,1)}, u32[]{:S(2)}, u32[]{:S(2)}) collective-permute-start(bf16[4,256,256]{2,1,0:T(8,128)(2,1)S(1)} %get-tuple-element.8.own_ref), channel_id=1, source_target_pairs={{0,1},{1,2},{2,3},{3,4},{4,5},{5,6},{6,7},{7,8},{8,9},{9,10},{10,1... | collective-permute-start | bytes 1572872 | tf_op jit(solution)/shard_map/ppermute | solution.py:15
  48.1 0.0 collective-permute-done.2.prev_ref
  48.1 12.7 %shard_map.56 = bf16[4,256,256]{2,1,0:T(8,128)(2,1)} custom-call(s32[12]{0:T(128)} %deltas_ref.7, s32[1]{0:T(128)S(6)} %copy.6.count_ref, bf16[4,256,256]{2,1,0:T(8,128)(2,1)} %collective-permute-done.2.prev_ref, bf16[4,256,256]{2,1,0:T(8,128)(2,1)} %copy-done.2, bf16[4,256,256]{2,1,0:T(8,128)(2,1)} %copy-done.8, bf16[12,256,256]{2,1,0:T(8,128)(2,1)} %left_ref.7, ...), custom_call_target="tpu_custom_call" | custom-call | flops 3221225472 | bytes 5242880 | tf_op jit(solution)/shard_map/pallas_call | solution.py:58
  60.8 0.0 collective-permute-done.7.next_ref
  60.8 0.0 collective-permute-done.6.prev_ref
  60.9 0.8 copy-done.7
  61.6 12.7 %shard_map.58 = bf16[4,256,256]{2,1,0:T(8,128)(2,1)} custom-call(s32[12]{0:T(128)} %deltas_ref.7, s32[1]{0:T(128)S(6)} %copy.6.count_ref, bf16[4,256,256]{2,1,0:T(8,128)(2,1)} %collective-permute-done.6.prev_ref, bf16[4,256,256]{2,1,0:T(8,128)(2,1)} %copy-done.1, bf16[4,256,256]{2,1,0:T(8,128)(2,1)} %copy-done.7, bf16[12,256,256]{2,1,0:T(8,128)(2,1)} %left_ref.7, ...), custom_call_target="tpu_custom_call" | custom-call | flops 3221225472 | bytes 5242880 | tf_op jit(solution)/shard_map/pallas_call | solution.py:58
  74.4 0.0 collective-permute-done.4.prev_ref
  74.4 12.9 %shard_map.57 = bf16[4,256,256]{2,1,0:T(8,128)(2,1)} custom-call(s32[12]{0:T(128)} %deltas_ref.7, s32[1]{0:T(128)S(6)} %copy.6.count_ref, bf16[4,256,256]{2,1,0:T(8,128)(2,1)} %collective-permute-done.4.prev_ref, bf16[4,256,256]{2,1,0:T(8,128)(2,1)} %copy-done, bf16[4,256,256]{2,1,0:T(8,128)(2,1)} %collective-permute-done.5.next_ref, ...), custom_call_target="tpu_custom_call" | custom-call | flops 3221225472 | bytes 5242880 | tf_op jit(solution)/shard_map/pallas_call | solution.py:58
  87.3 2.6 %maximum_bitcast_fusion = bf16[1,16,256,256]{3,2,1,0:T(8,128)(2,1)} fusion(bf16[4,256,256]{2,1,0:T(8,128)(2,1)S(1)} %copy-done.6, bf16[4,256,256]{2,1,0:T(8,128)(2,1)} %shard_map.57, bf16[4,256,256]{2,1,0:T(8,128)(2,1)S(1)} %copy-done.5, bf16[4,256,256]{2,1,0:T(8,128)(2,1)S(1)} %copy-done.4), kind=kLoop, calls=%fused_computation | loop fusion | flops 3145728 | bytes 4194304 | tf_op jit(solution)/shard_map/broadcast_in_dim | solution.py:84
  (20 shorter events, 0.0 us)
Async XLA Ops:
  1.7 31.7 %copy-start.3 = (bf16[4,256,256]{2,1,0:T(8,128)(2,1)}, bf16[4,256,256]{2,1,0:T(8,128)(2,1)S(1)}, u32[]{:S(2)}) copy-start(bf16[4,256,256]{2,1,0:T(8,128)(2,1)S(1)} %get-tuple-element.5.own_ref) | copy-start | bytes 1572868
  1.7 44.4 %copy-start.1 = (bf16[4,256,256]{2,1,0:T(8,128)(2,1)}, bf16[4,256,256]{2,1,0:T(8,128)(2,1)S(1)}, u32[]{:S(2)}) copy-start(bf16[4,256,256]{2,1,0:T(8,128)(2,1)S(1)} %get-tuple-element.7.own_ref) | copy-start | bytes 1572868
  1.7 44.4 %copy-start.2 = (bf16[4,256,256]{2,1,0:T(8,128)(2,1)}, bf16[4,256,256]{2,1,0:T(8,128)(2,1)S(1)}, u32[]{:S(2)}) copy-start(bf16[4,256,256]{2,1,0:T(8,128)(2,1)S(1)} %get-tuple-element.6.own_ref) | copy-start | bytes 1572868
  1.7 44.4 %copy-start = (bf16[4,256,256]{2,1,0:T(8,128)(2,1)}, bf16[4,256,256]{2,1,0:T(8,128)(2,1)S(1)}, u32[]{:S(2)}) copy-start(bf16[4,256,256]{2,1,0:T(8,128)(2,1)S(1)} %get-tuple-element.8.own_ref) | copy-start | bytes 1572868
  1.7 15.5 %collective-permute-start.1 = (bf16[4,256,256]{2,1,0:T(8,128)(2,1)S(1)}, bf16[4,256,256]{2,1,0:T(8,128)(2,1)S(1)}, u32[]{:S(2)}, u32[]{:S(2)}) collective-permute-start(bf16[4,256,256]{2,1,0:T(8,128)(2,1)S(1)} %get-tuple-element.5.own_ref), channel_id=1, source_target_pairs={{1,0},{2,1},{3,2},{4,3},{5,4},{6,5},{7,6},{8,7},{9,8},{10,9},{11,1... | collective-permute-start | bytes 1572872 | tf_op jit(solution)/shard_map/ppermute | solution.py:16
  4.3 17.5 %collective-permute-start = (bf16[4,256,256]{2,1,0:T(8,128)(2,1)S(1)}, bf16[4,256,256]{2,1,0:T(8,128)(2,1)S(1)}, u32[]{:S(2)}, u32[]{:S(2)}) collective-permute-start(bf16[4,256,256]{2,1,0:T(8,128)(2,1)S(1)} %get-tuple-element.5.own_ref), channel_id=1, source_target_pairs={{0,1},{1,2},{2,3},{3,4},{4,5},{5,6},{6,7},{7,8},{8,9},{9,10},{10,1... | collective-permute-start | bytes 1572872 | tf_op jit(solution)/shard_map/ppermute | solution.py:15
  8.2 37.9 %collective-permute-start.3 = (bf16[4,256,256]{2,1,0:T(8,128)(2,1)S(1)}, bf16[4,256,256]{2,1,0:T(8,128)(2,1)S(1)}, u32[]{:S(2)}, u32[]{:S(2)}) collective-permute-start(bf16[4,256,256]{2,1,0:T(8,128)(2,1)S(1)} %get-tuple-element.6.own_ref), channel_id=1, source_target_pairs={{1,0},{2,1},{3,2},{4,3},{5,4},{6,5},{7,6},{8,7},{9,8},{10,9},{11,1... | collective-permute-start | bytes 1572872 | tf_op jit(solution)/shard_map/ppermute | solution.py:16
  10.1 38.0 %collective-permute-start.2 = (bf16[4,256,256]{2,1,0:T(8,128)(2,1)S(1)}, bf16[4,256,256]{2,1,0:T(8,128)(2,1)}, u32[]{:S(2)}, u32[]{:S(2)}) collective-permute-start(bf16[4,256,256]{2,1,0:T(8,128)(2,1)S(1)} %get-tuple-element.6.own_ref), channel_id=1, source_target_pairs={{0,1},{1,2},{2,3},{3,4},{4,5},{5,6},{6,7},{7,8},{8,9},{9,10},{10,1... | collective-permute-start | bytes 1572872 | tf_op jit(solution)/shard_map/ppermute | solution.py:15
  14.7 46.2 %collective-permute-start.7 = (bf16[4,256,256]{2,1,0:T(8,128)(2,1)S(1)}, bf16[4,256,256]{2,1,0:T(8,128)(2,1)S(1)}, u32[]{:S(2)}, u32[]{:S(2)}) collective-permute-start(bf16[4,256,256]{2,1,0:T(8,128)(2,1)S(1)} %get-tuple-element.7.own_ref), channel_id=1, source_target_pairs={{1,0},{2,1},{3,2},{4,3},{5,4},{6,5},{7,6},{8,7},{9,8},{10,9},{11,1... | collective-permute-start | bytes 1572872 | tf_op jit(solution)/shard_map/ppermute | solution.py:16
  17.3 4.6 %copy-start.9 = (bf16[4,256,256]{2,1,0:T(8,128)(2,1)}, bf16[4,256,256]{2,1,0:T(8,128)(2,1)S(1)}, u32[]{:S(2)}) copy-start(bf16[4,256,256]{2,1,0:T(8,128)(2,1)S(1)} %collective-permute-done.1.next_ref) | copy-start | bytes 1572868
  17.3 43.6 %collective-permute-start.6 = (bf16[4,256,256]{2,1,0:T(8,128)(2,1)S(1)}, bf16[4,256,256]{2,1,0:T(8,128)(2,1)}, u32[]{:S(2)}, u32[]{:S(2)}) collective-permute-start(bf16[4,256,256]{2,1,0:T(8,128)(2,1)S(1)} %get-tuple-element.7.own_ref), channel_id=1, source_target_pairs={{0,1},{1,2},{2,3},{3,4},{4,5},{5,6},{6,7},{7,8},{8,9},{9,10},{10,1... | collective-permute-start | bytes 1572872 | tf_op jit(solution)/shard_map/ppermute | solution.py:15
  21.8 0.8 copy-start.10
  22.6 51.7 %collective-permute-start.5 = (bf16[4,256,256]{2,1,0:T(8,128)(2,1)S(1)}, bf16[4,256,256]{2,1,0:T(8,128)(2,1)}, u32[]{:S(2)}, u32[]{:S(2)}) collective-permute-start(bf16[4,256,256]{2,1,0:T(8,128)(2,1)S(1)} %get-tuple-element.8.own_ref), channel_id=1, source_target_pairs={{1,0},{2,1},{3,2},{4,3},{5,4},{6,5},{7,6},{8,7},{9,8},{10,9},{11,1... | collective-permute-start | bytes 1572872 | tf_op jit(solution)/shard_map/ppermute | solution.py:16
  46.1 2.0 %copy-start.8 = (bf16[4,256,256]{2,1,0:T(8,128)(2,1)}, bf16[4,256,256]{2,1,0:T(8,128)(2,1)S(1)}, u32[]{:S(2)}) copy-start(bf16[4,256,256]{2,1,0:T(8,128)(2,1)S(1)} %collective-permute-done.3.next_ref) | copy-start | bytes 1572868
  46.1 28.2 %collective-permute-start.4 = (bf16[4,256,256]{2,1,0:T(8,128)(2,1)S(1)}, bf16[4,256,256]{2,1,0:T(8,128)(2,1)}, u32[]{:S(2)}, u32[]{:S(2)}) collective-permute-start(bf16[4,256,256]{2,1,0:T(8,128)(2,1)S(1)} %get-tuple-element.8.own_ref), channel_id=1, source_target_pairs={{0,1},{1,2},{2,3},{3,4},{4,5},{5,6},{6,7},{7,8},{8,9},{9,10},{10,1... | collective-permute-start | bytes 1572872 | tf_op jit(solution)/shard_map/ppermute | solution.py:15
  60.8 0.8 copy-start.7
  74.4 12.9 %copy-start.4 = (bf16[4,256,256]{2,1,0:T(8,128)(2,1)S(1)}, bf16[4,256,256]{2,1,0:T(8,128)(2,1)}, u32[]{:S(2)}) copy-start(bf16[4,256,256]{2,1,0:T(8,128)(2,1)} %shard_map.55) | copy-start | bytes 1572868
  74.4 12.9 %copy-start.5 = (bf16[4,256,256]{2,1,0:T(8,128)(2,1)S(1)}, bf16[4,256,256]{2,1,0:T(8,128)(2,1)}, u32[]{:S(2)}) copy-start(bf16[4,256,256]{2,1,0:T(8,128)(2,1)} %shard_map.56) | copy-start | bytes 1572868
  74.4 12.9 %copy-start.6 = (bf16[4,256,256]{2,1,0:T(8,128)(2,1)S(1)}, bf16[4,256,256]{2,1,0:T(8,128)(2,1)}, u32[]{:S(2)}) copy-start(bf16[4,256,256]{2,1,0:T(8,128)(2,1)} %shard_map.58) | copy-start | bytes 1572868

commit v3 on v2

v3 whole, which is shorter than its diff:
```python
import functools

import jax
import jax.numpy as jnp
from jax import lax
from jax.experimental import pallas as pl
from jax.experimental.pallas import tpu as pltpu
from jax.sharding import PartitionSpec as P


def pair_kernel(deltas_ref, count_ref, table_ref, s0, s1, s2, s3, left_ref, right_ref, out_ref, acc_ref, mixed_ref):
    k = pl.program_id(0)
    rows, width = s0.shape[0], s0.shape[1]

    @pl.when(k == 0)
    def _():
        acc_ref[...] = jnp.zeros_like(acc_ref)

    @pl.when(k < count_ref[0])
    def _():
        which = table_ref[deltas_ref[k] + 1]
        left = left_ref[0]

        def run(src_ref):
            for r in range(rows):
                mixed_ref[pl.ds(r * width, width), :] = jnp.dot(
                    left, src_ref[r], preferred_element_type=jnp.float32
                ).astype(jnp.bfloat16)

        for m, ref in enumerate((s0, s1, s2, s3)):
            pl.when(which == m)(functools.partial(run, ref))
        acc_ref[...] += lax.dot_general(
            mixed_ref[...], right_ref[0], (((1,), (1,)), ((), ())), preferred_element_type=jnp.float32
        )

    @pl.when(k == pl.num_programs(0) - 1)
    def _():
        for r in range(rows):
            out_ref[r] = acc_ref[pl.ds(r * width, width), :].astype(out_ref.dtype)


def apply_pairs(sources, left_ops, right_ops, deltas, count, table):
    rows, width = sources[0].shape[0], sources[0].shape[1]
    slots = left_ops.shape[0]
    whole = pl.BlockSpec((rows, width, width), lambda k, d, c, t: (0, 0, 0))
    per_slot = pl.BlockSpec((1, width, width), lambda k, d, c, t: (jnp.minimum(k, c[0] - 1), 0, 0))
    flops = 4 * slots * rows * width ** 3
    moved = 2 * (4 * rows * width * width + 2 * slots * width * width + rows * width * width)
    return pl.pallas_call(
        pair_kernel,
        out_shape=jax.ShapeDtypeStruct((rows, width, width), jnp.bfloat16),
        grid_spec=pltpu.PrefetchScalarGridSpec(
            num_scalar_prefetch=3,
            grid=(slots,),
            in_specs=[whole] * 4 + [per_slot, per_slot],
            out_specs=whole,
            scratch_shapes=[
                pltpu.VMEM((rows * width, width), jnp.float32),
                pltpu.VMEM((rows * width, width), jnp.bfloat16),
            ],
        ),
        cost_estimate=pl.CostEstimate(flops=flops, bytes_accessed=moved, transcendentals=0),
    )(deltas, count, table, *sources, left_ops, right_ops)


def on_device(wave, left_ops, right_ops, deltas, counts):
    n = lax.axis_size("sector")
    me = lax.axis_index("sector")
    parity = me % 2
    own = wave[0]
    half = own.shape[0] // 2
    mine = lax.dynamic_slice_in_dim(own, parity * half, half, 0)
    other = lax.dynamic_slice_in_dim(own, (1 - parity) * half, half, 0)

    odd, even = range(1, n, 2), range(0, n, 2)
    near = [(j, j + 1) for j in odd if j + 1 < n] + [(j, j - 1) for j in even if j >= 2]
    far = [(j, j + 2) for j in odd if j + 2 < n] + [(j, j - 2) for j in even if j >= 2]
    partner = [(j, j ^ 1) for j in range(n)]

    from_near = lax.ppermute(other, "sector", near)
    from_far = lax.ppermute(mine, "sector", far)
    from_partner = lax.ppermute(other, "sector", partner)
    sources = (mine, from_near, from_far, from_partner)

    left_p = lax.ppermute(left_ops, "sector", partner)
    right_p = lax.ppermute(right_ops, "sector", partner)
    deltas_p = lax.ppermute(deltas, "sector", partner)
    counts_p = lax.ppermute(counts, "sector", partner)

    key = 1 + parity
    steps = jnp.arange(3, dtype=jnp.int32)
    own_table = lax.bitwise_xor(steps + parity, key).astype(jnp.int32)
    partner_table = lax.bitwise_xor(steps + 1 - parity, key).astype(jnp.int32)

    own_half = apply_pairs(sources, left_ops, right_ops, deltas, counts, own_table)
    partner_half = apply_pairs(sources, left_p, right_p, deltas_p, counts_p, partner_table)
    returned = lax.ppermute(partner_half, "sector", partner)

    out = jnp.zeros_like(own)
    out = lax.dynamic_update_slice_in_dim(out, own_half, parity * half, 0)
    out = lax.dynamic_update_slice_in_dim(out, returned, (1 - parity) * half, 0)
    return out[None]


def solution(mesh):
    return jax.shard_map(
        on_device,
        mesh=mesh,
        in_specs=(
            P(("group", "sector"), None, None, None),
            P(("group", "sector"), None, None),
            P(("group", "sector"), None, None),
            P(("group", "sector")),
            P(("group", "sector")),
        ),
        out_specs=P(("group", "sector"), None, None, None),
        check_vma=False,
    )
```

time: 91.7 us -> 90.6 us (0.988)
  the two profiles are of different devices: /device:TPU:23 before, /device:TPU:0 now
where the time goes in v3:
time: 90.6 us; the launch traced here: 89.9 us
  starting transfers between devices  40.8 us (45%)
  Pallas kernels  23.1 us (25%)
  waiting for transfers between devices  18.7 us (21%)
  local copies, waits for them, and re-layouts  5.34 us (6%)
  other arithmetic  1.17 us (1%)
    ppermute x1, starting transfers between devices, on_device(): returned = lax.ppermute(partner_half, 'sector', partner)  30.6 us
    pallas_call x2, Pallas kernels, apply_pairs(): pl.pallas_call(pair_kernel, out_shape=jax.ShapeDtypeStruct((rows, width,...  23.1 us
    ppermute x1, waiting for transfers between devices, on_device(): from_far = lax.ppermute(mine, 'sector', far)  16.9 us
    ppermute x1, starting transfers between devices, on_device(): counts_p = lax.ppermute(counts, 'sector', partner)  7.1 us
    unnamed x12, local copies, waits for them, and re-layouts  2.34 us
  transfers between devices with their start and end apart: 8, of which 3 were waited for; matrix products, arithmetic and copies ran while one was open for 3% of the time, Pallas kernels for 18%

profile of v3, /device:TPU:0, one launch (start us, length us, event | category | flops | bytes accessed | tf_op | source)
XLA Modules:
  0.0 89.9 jit_solution(12994283141207526183)
XLA Ops:
  0.0 0.5 collective-permute-start.5
  0.5 0.1 collective-permute-start.6
  0.5 1.7 %dynamic-slice_bitcast_fusion = (bf16[8,256,256]{2,1,0:T(8,128)(2,1)S(1)}, bf16[8,256,256]{2,1,0:T(8,128)(2,1)S(1)}) fusion(bf16[1,16,256,256]{3,2,1,0:T(8,128)(2,1)} %param.5, s32[]{:T(128)S(6)} %select_n.17, s32[]{:T(128)S(6)} %select_n.16), kind=kLoop, calls=%fused_computation.2 | loop fusion | bytes 4194312 | tf_op jit(solution)/shard_map/dynamic_slice | solution.py:73
  2.2 0.0 copy-start.1
  2.2 0.7 collective-permute-start
  3.0 1.3 %collective-permute-start.1 = (bf16[8,256,256]{2,1,0:T(8,128)(2,1)S(1)}, bf16[8,256,256]{2,1,0:T(8,128)(2,1)}, u32[]{:S(2)}, u32[]{:S(2)}) collective-permute-start(bf16[8,256,256]{2,1,0:T(8,128)(2,1)S(1)} %get-tuple-element.6.s0), channel_id=1, source_target_pairs={{1,3},{3,5},{5,7},{7,9},{9,11},{11,13},{13,15},{2,0},{4,2},{6,4},{... | collective-permute-start | bytes 3145736 | tf_op jit(solution)/shard_map/ppermute | solution.py:81
  4.3 7.1 %collective-permute-start.4 = (s32[1]{0:T(128)}, s32[1]{0:T(128)}, u32[]{:S(2)}, u32[]{:S(2)}) collective-permute-start(s32[1]{0:T(128)} %param.9), channel_id=1, source_target_pairs={{0,1},{1,0},{2,3},{3,2},{4,5},{5,4},{6,7},{7,6},{8,9},{9,8},{10,11... | collective-permute-start | bytes 20 | tf_op jit(solution)/shard_map/ppermute | solution.py:88
  11.4 1.0 %collective-permute-done.4.count_ref = s32[1]{0:T(128)} collective-permute-done((s32[1]{0:T(128)}, s32[1]{0:T(128)}, u32[]{:S(2)}, u32[]{:S(2)}) %collective-permute-start.4) | collective-permute-done | bytes 36 | tf_op jit(solution)/shard_map/ppermute | solution.py:88
  12.3 0.3 collective-permute-start.3
  12.6 0.8 collective-permute-done.3.deltas_ref
  13.4 0.3 collective-permute-start.2
  13.7 0.6 subtract_xor_fusion.table_ref
  14.3 0.0 collective-permute-done.s1
  14.3 16.9 %collective-permute-done.1.s2 = bf16[8,256,256]{2,1,0:T(8,128)(2,1)} collective-permute-done((bf16[8,256,256]{2,1,0:T(8,128)(2,1)S(1)}, bf16[8,256,256]{2,1,0:T(8,128)(2,1)}, u32[]{:S(2)}, u32[]{:S(2)}) %collective-permute-start.1) | collective-permute-done | bytes 1048608 | tf_op jit(solution)/shard_map/ppermute | solution.py:81
  31.2 7.3 %shard_map.56 = bf16[8,256,256]{2,1,0:T(8,128)(2,1)} custom-call(s32[12]{0:T(128)} %copy-done.5, s32[1]{0:T(128)} %collective-permute-done.4.count_ref, s32[3]{0:T(128)} %subtract_xor_fusion.table_ref, bf16[8,256,256]{2,1,0:T(8,128)(2,1)} %copy-done.1, bf16[8,256,256]{2,1,0:T(8,128)(2,1)} %copy-done.3, bf16[8,256,256]{2,1,0:T(8,128)(2,1)} %collective-permute-done.1.s2, ...), custom_call_target="tpu_custom_call" | custom-call | flops 6442450944 | bytes 8388608 | tf_op jit(solution)/shard_map/pallas_call | solution.py:49
  38.6 30.6 %collective-permute-start.7 = (bf16[8,256,256]{2,1,0:T(8,128)(2,1)}, bf16[8,256,256]{2,1,0:T(8,128)(2,1)S(1)}, u32[]{:S(2)}, u32[]{:S(2)}) collective-permute-start(bf16[8,256,256]{2,1,0:T(8,128)(2,1)} %shard_map.56), channel_id=1, source_target_pairs={{0,1},{1,0},{2,3},{3,2},{4,5},{5,4},{6,7},{7,6},{8,9},{9,8},{10,11... | collective-permute-start | bytes 3145736 | tf_op jit(solution)/shard_map/ppermute | solution.py:97
  69.9 0.6 add_xor_fusion.table_ref
  70.5 15.8 %shard_map.55 = bf16[8,256,256]{2,1,0:T(8,128)(2,1)} custom-call(s32[12]{0:T(128)} %deltas_ref.1, s32[1]{0:T(128)S(6)} %copy.8.count_ref, s32[3]{0:T(128)} %add_xor_fusion.table_ref, bf16[8,256,256]{2,1,0:T(8,128)(2,1)} %copy-done.1, bf16[8,256,256]{2,1,0:T(8,128)(2,1)} %copy-done.3, bf16[8,256,256]{2,1,0:T(8,128)(2,1)} %collective-permute-done.1.s2, ...), custom_call_target="tpu_custom_call" | custom-call | flops 6442450944 | bytes 8388608 | tf_op jit(solution)/shard_map/pallas_call | solution.py:49
  86.3 0.2 broadcast_in_dim.8
  86.5 1.0 %copy-done.2 = bf16[8,256,256]{2,1,0:T(8,128)(2,1)S(1)} copy-done((bf16[8,256,256]{2,1,0:T(8,128)(2,1)S(1)}, bf16[8,256,256]{2,1,0:T(8,128)(2,1)}, u32[]{:S(2)}) %copy-start.2) | copy-done | bytes 1048600
  87.5 0.1 bitcast_dynamic-update-slice_fusion.1
  87.6 0.0 copy-start
  87.6 1.3 %copy-done = bf16[1,16,256,256]{3,2,1,0:T(8,128)(2,1)} copy-done((bf16[1,16,256,256]{3,2,1,0:T(8,128)(2,1)}, bf16[1,16,256,256]{3,2,1,0:T(8,128)(2,1)S(1)}, u32[]{:S(2)}) %copy-start) | copy-done | bytes 2097176
  88.9 1.0 %bitcast_dynamic-update-slice_fusion = bf16[1,16,256,256]{3,2,1,0:T(8,128)(2,1)} fusion(bf16[1,16,256,256]{3,2,1,0:T(8,128)(2,1)} %copy-done, s32[]{:T(128)S(6)} %select_n.17, bf16[8,256,256]{2,1,0:T(8,128)(2,1)S(1)} %collective-permute-done.7), kind=kLoop, calls=%fused_computation | loop fusion | bytes 2097156 | tf_op jit(solution)/shard_map/dynamic_update_slice | solution.py:101
  (12 shorter events, 0.0 us)
Async XLA Ops:
  0.0 31.2 %collective-permute-start.5 = (bf16[12,256,256]{2,1,0:T(8,128)(2,1)}, bf16[12,256,256]{2,1,0:T(8,128)(2,1)}, u32[]{:S(2)}, u32[]{:S(2)}) collective-permute-start(bf16[12,256,256]{2,1,0:T(8,128)(2,1)} %left_ref.1), channel_id=1, source_target_pairs={{0,1},{1,0},{2,3},{3,2},{4,5},{5,4},{6,7},{7,6},{8,9},{9,8},{10,11... | collective-permute-start | bytes 4718600 | tf_op jit(solution)/shard_map/ppermute | solution.py:85
  0.5 30.8 %collective-permute-start.6 = (bf16[12,256,256]{2,1,0:T(8,128)(2,1)}, bf16[12,256,256]{2,1,0:T(8,128)(2,1)}, u32[]{:S(2)}, u32[]{:S(2)}) collective-permute-start(bf16[12,256,256]{2,1,0:T(8,128)(2,1)} %right_ref.1), channel_id=1, source_target_pairs={{0,1},{1,0},{2,3},{3,2},{4,5},{5,4},{6,7},{7,6},{8,9},{9,8},{10,11... | collective-permute-start | bytes 4718600 | tf_op jit(solution)/shard_map/ppermute | solution.py:86
  0.5 11.8 %copy-start.4 = (s32[12]{0:T(128)S(1)}, s32[12]{0:T(128)}, u32[]{:S(2)}) copy-start(s32[12]{0:T(128)} %deltas_ref.1) | copy-start | bytes 148
  2.2 29.0 %copy-start.1 = (bf16[8,256,256]{2,1,0:T(8,128)(2,1)}, bf16[8,256,256]{2,1,0:T(8,128)(2,1)S(1)}, u32[]{:S(2)}) copy-start(bf16[8,256,256]{2,1,0:T(8,128)(2,1)S(1)} %get-tuple-element.6.s0) | copy-start | bytes 3145732
  2.2 12.1 %collective-permute-start = (bf16[8,256,256]{2,1,0:T(8,128)(2,1)S(1)}, bf16[8,256,256]{2,1,0:T(8,128)(2,1)S(1)}, u32[]{:S(2)}, u32[]{:S(2)}) collective-permute-start(bf16[8,256,256]{2,1,0:T(8,128)(2,1)S(1)} %get-tuple-element.5), channel_id=1, source_target_pairs={{1,2},{3,4},{5,6},{7,8},{9,10},{11,12},{13,14},{2,1},{4,3},{6,5},{... | collective-permute-start | bytes 3145736 | tf_op jit(solution)/shard_map/ppermute | solution.py:80
  3.0 28.3 %collective-permute-start.1 = (bf16[8,256,256]{2,1,0:T(8,128)(2,1)S(1)}, bf16[8,256,256]{2,1,0:T(8,128)(2,1)}, u32[]{:S(2)}, u32[]{:S(2)}) collective-permute-start(bf16[8,256,256]{2,1,0:T(8,128)(2,1)S(1)} %get-tuple-element.6.s0), channel_id=1, source_target_pairs={{1,3},{3,5},{5,7},{7,9},{9,11},{11,13},{13,15},{2,0},{4,2},{6,4},{... | collective-permute-start | bytes 3145736 | tf_op jit(solution)/shard_map/ppermute | solution.py:81
  4.3 8.1 %collective-permute-start.4 = (s32[1]{0:T(128)}, s32[1]{0:T(128)}, u32[]{:S(2)}, u32[]{:S(2)}) collective-permute-start(s32[1]{0:T(128)} %param.9), channel_id=1, source_target_pairs={{0,1},{1,0},{2,3},{3,2},{4,5},{5,4},{6,7},{7,6},{8,9},{9,8},{10,11... | collective-permute-start | bytes 20 | tf_op jit(solution)/shard_map/ppermute | solution.py:88
  12.3 1.1 %collective-permute-start.3 = (s32[12]{0:T(128)S(1)}, s32[12]{0:T(128)S(1)}, u32[]{:S(2)}, u32[]{:S(2)}) collective-permute-start(s32[12]{0:T(128)S(1)} %copy-done.4), channel_id=1, source_target_pairs={{0,1},{1,0},{2,3},{3,2},{4,5},{5,4},{6,7},{7,6},{8,9},{9,8},{10,11... | collective-permute-start | bytes 152 | tf_op jit(solution)/shard_map/ppermute | solution.py:87
  13.4 17.8 %copy-start.5 = (s32[12]{0:T(128)}, s32[12]{0:T(128)S(1)}, u32[]{:S(2)}) copy-start(s32[12]{0:T(128)S(1)} %collective-permute-done.3.deltas_ref) | copy-start | bytes 148
  13.4 17.8 %collective-permute-start.2 = (bf16[8,256,256]{2,1,0:T(8,128)(2,1)S(1)}, bf16[8,256,256]{2,1,0:T(8,128)(2,1)}, u32[]{:S(2)}, u32[]{:S(2)}) collective-permute-start(bf16[8,256,256]{2,1,0:T(8,128)(2,1)S(1)} %get-tuple-element.5), channel_id=1, source_target_pairs={{0,1},{1,0},{2,3},{3,2},{4,5},{5,4},{6,7},{7,6},{8,9},{9,8},{10,11... | collective-permute-start | bytes 3145736 | tf_op jit(solution)/shard_map/ppermute | solution.py:82
  14.3 16.9 %copy-start.3 = (bf16[8,256,256]{2,1,0:T(8,128)(2,1)}, bf16[8,256,256]{2,1,0:T(8,128)(2,1)S(1)}, u32[]{:S(2)}) copy-start(bf16[8,256,256]{2,1,0:T(8,128)(2,1)S(1)} %collective-permute-done.s1) | copy-start | bytes 3145732
  38.6 49.0 %collective-permute-start.7 = (bf16[8,256,256]{2,1,0:T(8,128)(2,1)}, bf16[8,256,256]{2,1,0:T(8,128)(2,1)S(1)}, u32[]{:S(2)}, u32[]{:S(2)}) collective-permute-start(bf16[8,256,256]{2,1,0:T(8,128)(2,1)} %shard_map.56), channel_id=1, source_target_pairs={{0,1},{1,0},{2,3},{3,2},{4,5},{5,4},{6,7},{7,6},{8,9},{9,8},{10,11... | collective-permute-start | bytes 3145736 | tf_op jit(solution)/shard_map/ppermute | solution.py:97
  86.3 1.2 %copy-start.2 = (bf16[8,256,256]{2,1,0:T(8,128)(2,1)S(1)}, bf16[8,256,256]{2,1,0:T(8,128)(2,1)}, u32[]{:S(2)}) copy-start(bf16[8,256,256]{2,1,0:T(8,128)(2,1)} %shard_map.55) | copy-start | bytes 3145732
  87.6 1.3 %copy-start = (bf16[1,16,256,256]{3,2,1,0:T(8,128)(2,1)}, bf16[1,16,256,256]{3,2,1,0:T(8,128)(2,1)S(1)}, u32[]{:S(2)}) copy-start(bf16[1,16,256,256]{3,2,1,0:T(8,128)(2,1)S(1)} %bitcast_dynamic-update-slice_fusion.1) | copy-start | bytes 6291460

commit v4 on v3

--- a/solution.py
+++ b/solution.py
@@ -8,17 +8,26 @@
 from jax.sharding import PartitionSpec as P
 
 
-def pair_kernel(deltas_ref, count_ref, table_ref, s0, s1, s2, s3, left_ref, right_ref, out_ref, acc_ref, mixed_ref):
+def pair_kernel(deltas_ref, count_ref, table_ref, sa, sb, left_ref, right_ref, *rest):
+    if len(rest) == 4:
+        start_ref, out_ref, acc_ref, mixed_ref = rest
+    else:
+        start_ref = None
+        out_ref, acc_ref, mixed_ref = rest
     k = pl.program_id(0)
-    rows, width = s0.shape[0], s0.shape[1]
+    rows, width = sa.shape[0], sa.shape[1]
 
     @pl.when(k == 0)
     def _():
-        acc_ref[...] = jnp.zeros_like(acc_ref)
+        if start_ref is None:
+            acc_ref[...] = jnp.zeros_like(acc_ref)
+        else:
+            acc_ref[...] = start_ref[...]
 
-    @pl.when(k < count_ref[0])
+    which = table_ref[jnp.clip(deltas_ref[k], -1, 1) + 1]
+
+    @pl.when(jnp.logical_and(k < count_ref[0], which < 2))
     def _():
-        which = table_ref[deltas_ref[k] + 1]
         left = left_ref[0]
 
         def run(src_ref):
@@ -27,7 +36,7 @@
                     left, src_ref[r], preferred_element_type=jnp.float32
                 ).astype(jnp.bfloat16)
 
-        for m, ref in enumerate((s0, s1, s2, s3)):
+        for m, ref in enumerate((sa, sb)):
             pl.when(which == m)(functools.partial(run, ref))
         acc_ref[...] += lax.dot_general(
             mixed_ref[...], right_ref[0], (((1,), (1,)), ((), ())), preferred_element_type=jnp.float32
@@ -35,32 +44,34 @@
 
     @pl.when(k == pl.num_programs(0) - 1)
     def _():
-        for r in range(rows):
-            out_ref[r] = acc_ref[pl.ds(r * width, width), :].astype(out_ref.dtype)
+        out_ref[...] = acc_ref[...].astype(out_ref.dtype)
 
 
-def apply_pairs(sources, left_ops, right_ops, deltas, count, table):
+def apply_pairs(sources, left_ops, right_ops, deltas, count, table, start=None):
     rows, width = sources[0].shape[0], sources[0].shape[1]
     slots = left_ops.shape[0]
     whole = pl.BlockSpec((rows, width, width), lambda k, d, c, t: (0, 0, 0))
+    flat = pl.BlockSpec((rows * width, width), lambda k, d, c, t: (0, 0))
     per_slot = pl.BlockSpec((1, width, width), lambda k, d, c, t: (jnp.minimum(k, c[0] - 1), 0, 0))
-    flops = 4 * slots * rows * width ** 3
-    moved = 2 * (4 * rows * width * width + 2 * slots * width * width + rows * width * width)
+    flops = 4 * slots * rows * width ** 3 // 2
+    moved = 2 * (2 * rows * width * width + 2 * slots * width * width) + 6 * rows * width * width
+    extra = () if start is None else (start,)
+    dtype = jnp.float32 if start is None else jnp.bfloat16
     return pl.pallas_call(
         pair_kernel,
-        out_shape=jax.ShapeDtypeStruct((rows, width, width), jnp.bfloat16),
+        out_shape=jax.ShapeDtypeStruct((rows * width, width), dtype),
         grid_spec=pltpu.PrefetchScalarGridSpec(
             num_scalar_prefetch=3,
             grid=(slots,),
-            in_specs=[whole] * 4 + [per_slot, per_slot],
-            out_specs=whole,
+            in_specs=[whole] * 2 + [per_slot, per_slot] + [flat] * len(extra),
+            out_specs=flat,
             scratch_shapes=[
                 pltpu.VMEM((rows * width, width), jnp.float32),
                 pltpu.VMEM((rows * width, width), jnp.bfloat16),
             ],
         ),
         cost_estimate=pl.CostEstimate(flops=flops, bytes_accessed=moved, transcendentals=0),
-    )(deltas, count, table, *sources, left_ops, right_ops)
+    )(deltas, count, table, *sources, left_ops, right_ops, *extra)
 
 
 def on_device(wave, left_ops, right_ops, deltas, counts):
@@ -89,11 +100,24 @@
 
     key = 1 + parity
     steps = jnp.arange(3, dtype=jnp.int32)
-    own_table = lax.bitwise_xor(steps + parity, key).astype(jnp.int32)
-    partner_table = lax.bitwise_xor(steps + 1 - parity, key).astype(jnp.int32)
+    own_ids = lax.bitwise_xor(steps + parity, key)
+    partner_ids = lax.bitwise_xor(steps + 1 - parity, key)
+    on_chip = jnp.array([0, 2, 2, 1], jnp.int32)
+    off_chip = jnp.array([2, 0, 1, 2], jnp.int32)
+    local = (mine, from_partner)
+    halos = (from_near, from_far)
+    shape = own.shape[1:]
 
-    own_half = apply_pairs(sources, left_ops, right_ops, deltas, counts, own_table)
-    partner_half = apply_pairs(sources, left_p, right_p, deltas_p, counts_p, partner_table)
+    partner_sum = apply_pairs(local, left_p, right_p, deltas_p, counts_p, on_chip[partner_ids])
+    own_sum = apply_pairs(local, left_ops, right_ops, deltas, counts, on_chip[own_ids])
+    own_sum, partner_sum, from_near, from_far = lax.optimization_barrier(
+        (own_sum, partner_sum, from_near, from_far)
+    )
+    halos = (from_near, from_far)
+    partner_half = apply_pairs(halos, left_p, right_p, deltas_p, counts_p, off_chip[partner_ids], partner_sum)
+    partner_half = partner_half.reshape((half,) + shape)
+    own_half = apply_pairs(halos, left_ops, right_ops, deltas, counts, off_chip[own_ids], own_sum)
+    own_half = own_half.reshape((half,) + shape)
     returned = lax.ppermute(partner_half, "sector", partner)
 
     out = jnp.zeros_like(own)

time: 90.6 us -> 86.9 us (0.959)
  the two profiles are of different devices: /device:TPU:0 before, /device:TPU:6 now
where the time goes in v4:
time: 86.9 us; the launch traced here: 85.5 us
  Pallas kernels  41.4 us (48%)
  starting transfers between devices  24.7 us (28%)
  local copies, waits for them, and re-layouts  11.6 us (13%)
  waiting for transfers between devices  6.97 us (8%)
    pallas_call x4, Pallas kernels, apply_pairs(): pl.pallas_call(pair_kernel, out_shape=jax.ShapeDtypeStruct((rows * width,...  41.4 us
    ppermute x1, starting transfers between devices, on_device(): returned = lax.ppermute(partner_half, 'sector', partner)  17.3 us
    ppermute x1, waiting for transfers between devices, on_device(): from_near = lax.ppermute(other, 'sector', near)  5.84 us
    unnamed x16, local copies, waits for them, and re-layouts  3.89 us
    ppermute x1, starting transfers between devices, on_device(): from_near = lax.ppermute(other, 'sector', near)  2.5 us
    ppermute x1, starting transfers between devices, on_device(): counts_p = lax.ppermute(counts, 'sector', partner)  2.27 us
    ppermute x1, starting transfers between devices, on_device(): from_far = lax.ppermute(mine, 'sector', far)  1.92 us
  transfers between devices with their start and end apart: 8, of which 2 were waited for; matrix products, arithmetic and copies ran while one was open for 8% of the time, Pallas kernels for 40%

profile of v4, /device:TPU:6, one launch (start us, length us, event | category | flops | bytes accessed | tf_op | source)
XLA Modules:
  0.0 85.5 jit_solution(8511477603819656438)
XLA Ops:
  0.0 0.5 collective-permute-start.4
  0.5 1.7 %dynamic-slice_bitcast_fusion = (bf16[8,256,256]{2,1,0:T(8,128)(2,1)S(1)}, bf16[8,256,256]{2,1,0:T(8,128)(2,1)S(1)}) fusion(bf16[1,16,256,256]{3,2,1,0:T(8,128)(2,1)} %param.7, s32[]{:T(128)S(6)} %select_n.40, s32[]{:T(128)S(6)} %select_n.39), kind=kLoop, calls=%fused_computation.5 | loop fusion | bytes 4194312 | tf_op jit(solution)/shard_map/dynamic_slice | solution.py:84
  2.2 0.1 collective-permute-start
  2.3 2.5 %collective-permute-start.5 = (bf16[8,256,256]{2,1,0:T(8,128)(2,1)S(1)}, bf16[8,256,256]{2,1,0:T(8,128)(2,1)S(1)}, u32[]{:S(2)}, u32[]{:S(2)}) collective-permute-start(bf16[8,256,256]{2,1,0:T(8,128)(2,1)S(1)} %get-tuple-element.13), channel_id=1, source_target_pairs={{1,2},{3,4},{5,6},{7,8},{9,10},{11,12},{13,14},{2,1},{4,3},{6,5},{... | collective-permute-start | bytes 3145736 | tf_op jit(solution)/shard_map/ppermute | solution.py:91
  4.8 1.9 %collective-permute-start.6 = (bf16[8,256,256]{2,1,0:T(8,128)(2,1)S(1)}, bf16[8,256,256]{2,1,0:T(8,128)(2,1)}, u32[]{:S(2)}, u32[]{:S(2)}) collective-permute-start(bf16[8,256,256]{2,1,0:T(8,128)(2,1)S(1)} %get-tuple-element.14.sa), channel_id=1, source_target_pairs={{1,3},{3,5},{5,7},{7,9},{9,11},{11,13},{13,15},{2,0},{4,2},{6,4},{... | collective-permute-start | bytes 3145736 | tf_op jit(solution)/shard_map/ppermute | solution.py:92
  6.8 1.2 %gather_fusion.2 = s32[3]{0:T(128)} fusion(s32[4]{0:T(128)S(1)} %copy-done.1, s32[1024]{0:T(1024)S(1)} %pad_clamp_fusion), kind=kCustom, calls=%fused_computation.2 | custom fusion | bytes 36 | tf_op jit(solution)/shard_map/gather | solution.py:111
  8.0 1.2 %gather_fusion.1 = s32[3]{0:T(128)} fusion(s32[4]{0:T(128)S(1)} %copy-done.1, s32[1024]{0:T(1024)S(1)} %pad_clamp_fusion.1), kind=kCustom, calls=%fused_computation.1 | custom fusion | bytes 36 | tf_op jit(solution)/shard_map/gather | solution.py:112
  9.8 1.1 %gather_fusion.3 = s32[3]{0:T(128)} fusion(s32[4]{0:T(128)S(1)} %copy-done, s32[1024]{0:T(1024)S(1)} %pad_clamp_fusion), kind=kCustom, calls=%fused_computation.3 | custom fusion | bytes 36 | tf_op jit(solution)/shard_map/gather | solution.py:117
  11.0 2.3 %collective-permute-start.2 = (s32[1]{0:T(128)}, s32[1]{0:T(128)}, u32[]{:S(2)}, u32[]{:S(2)}) collective-permute-start(s32[1]{0:T(128)} %param.11), channel_id=1, source_target_pairs={{0,1},{1,0},{2,3},{3,2},{4,5},{5,4},{6,7},{7,6},{8,9},{9,8},{10,11... | collective-permute-start | bytes 20 | tf_op jit(solution)/shard_map/ppermute | solution.py:99
  13.2 13.6 %shard_map.73.rest_0_ = f32[2048,256]{1,0:T(8,128)} custom-call(s32[12]{0:T(128)} %deltas_ref.3, s32[1]{0:T(128)S(6)} %copy.10.count_ref, s32[3]{0:T(128)} %gather_fusion.1, bf16[8,256,256]{2,1,0:T(8,128)(2,1)} %copy-done.3, bf16[8,256,256]{2,1,0:T(8,128)(2,1)} %collective-permute-done.sb, bf16[12,256,256]{2,1,0:T(8,128)(2,1)} %left_ref.3, ...), custom_call_target="tpu_custom_call" | custom-call | flops 3221225472 | bytes 8388608 | tf_op jit(solution)/shard_map/pallas_call | solution.py:60
  26.9 1.1 %collective-permute-done.1.deltas_ref = s32[12]{0:T(128)S(1)} collective-permute-done((s32[12]{0:T(128)S(1)}, s32[12]{0:T(128)S(1)}, u32[]{:S(2)}, u32[]{:S(2)}) %collective-permute-start.1) | collective-permute-done | bytes 80 | tf_op jit(solution)/shard_map/ppermute | solution.py:98
  28.0 0.5 copy-done.7
  28.5 6.5 %shard_map.74.rest_0_ = f32[2048,256]{1,0:T(8,128)} custom-call(s32[12]{0:T(128)} %copy-done.7, s32[1]{0:T(128)} %collective-permute-done.2.count_ref, s32[3]{0:T(128)} %gather_fusion.2, bf16[8,256,256]{2,1,0:T(8,128)(2,1)} %copy-done.3, bf16[8,256,256]{2,1,0:T(8,128)(2,1)} %collective-permute-done.sb, ...), custom_call_target="tpu_custom_call" | custom-call | flops 3221225472 | bytes 8388608 | tf_op jit(solution)/shard_map/pallas_call | solution.py:60
  35.1 5.8 %collective-permute-done.5.sa = bf16[8,256,256]{2,1,0:T(8,128)(2,1)S(1)} collective-permute-done((bf16[8,256,256]{2,1,0:T(8,128)(2,1)S(1)}, bf16[8,256,256]{2,1,0:T(8,128)(2,1)S(1)}, u32[]{:S(2)}, u32[]{:S(2)}) %collective-permute-start.5) | collective-permute-done | bytes 1048608 | tf_op jit(solution)/shard_map/ppermute | solution.py:91
  40.9 1.0 %copy-done.5 = bf16[8,256,256]{2,1,0:T(8,128)(2,1)} copy-done((bf16[8,256,256]{2,1,0:T(8,128)(2,1)}, bf16[8,256,256]{2,1,0:T(8,128)(2,1)S(1)}, u32[]{:S(2)}) %copy-start.5) | copy-done | bytes 1048600
  41.9 7.4 %shard_map.76 = bf16[2048,256]{1,0:T(8,128)(2,1)} custom-call(s32[12]{0:T(128)} %copy-done.7, s32[1]{0:T(128)} %collective-permute-done.2.count_ref, s32[3]{0:T(128)} %gather_fusion.3, bf16[8,256,256]{2,1,0:T(8,128)(2,1)} %copy-done.5, bf16[8,256,256]{2,1,0:T(8,128)(2,1)} %collective-permute-done.6.sb, ...), custom_call_target="tpu_custom_call" | custom-call | flops 3221225472 | bytes 8388608 | tf_op jit(solution)/shard_map/pallas_call | solution.py:60
  49.3 17.3 %collective-permute-start.7 = (bf16[8,256,256]{2,1,0:T(8,128)(2,1)}, bf16[8,256,256]{2,1,0:T(8,128)(2,1)S(1)}, u32[]{:S(2)}, u32[]{:S(2)}) collective-permute-start(bf16[8,256,256]{2,1,0:T(8,128)(2,1)} %bitcast.13), channel_id=1, source_target_pairs={{0,1},{1,0},{2,3},{3,2},{4,5},{5,4},{6,7},{7,6},{8,9},{9,8},{10,11... | collective-permute-start | bytes 3145736 | tf_op jit(solution)/shard_map/ppermute | solution.py:121
  66.7 1.2 %gather_fusion = s32[3]{0:T(128)} fusion(s32[4]{0:T(128)S(1)} %copy-done, s32[1024]{0:T(1024)S(1)} %pad_clamp_fusion.1), kind=kCustom, calls=%fused_computation | custom fusion | bytes 36 | tf_op jit(solution)/shard_map/gather | solution.py:119
  67.9 14.0 %shard_map.75 = bf16[2048,256]{1,0:T(8,128)(2,1)} custom-call(s32[12]{0:T(128)} %deltas_ref.3, s32[1]{0:T(128)S(6)} %copy.10.count_ref, s32[3]{0:T(128)} %gather_fusion, bf16[8,256,256]{2,1,0:T(8,128)(2,1)} %copy-done.5, bf16[8,256,256]{2,1,0:T(8,128)(2,1)} %collective-permute-done.6.sb, bf16[12,256,256]{2,1,0:T(8,128)(2,1)} %left_ref.3, ...), custom_call_target="tpu_custom_call" | custom-call | flops 3221225472 | bytes 8388608 | tf_op jit(solution)/shard_map/pallas_call | solution.py:60
  81.8 0.2 broadcast_in_dim.12
  82.0 1.0 %copy-done.4 = bf16[2048,256]{1,0:T(8,128)(2,1)S(1)} copy-done((bf16[2048,256]{1,0:T(8,128)(2,1)S(1)}, bf16[2048,256]{1,0:T(8,128)(2,1)}, u32[]{:S(2)}) %copy-start.4) | copy-done | bytes 1048600
  83.1 0.1 constant_dynamic-update-slice_fusion
  83.2 1.3 %copy-done.2 = bf16[1,16,256,256]{3,2,1,0:T(8,128)(2,1)} copy-done((bf16[1,16,256,256]{3,2,1,0:T(8,128)(2,1)}, bf16[1,16,256,256]{3,2,1,0:T(8,128)(2,1)S(1)}, u32[]{:S(2)}) %copy-start.2) | copy-done | bytes 2097176
  84.5 1.0 %bitcast_dynamic-update-slice_fusion = bf16[1,16,256,256]{3,2,1,0:T(8,128)(2,1)} fusion(bf16[1,16,256,256]{3,2,1,0:T(8,128)(2,1)} %copy-done.2, s32[]{:T(128)S(6)} %select_n.40, bf16[8,256,256]{2,1,0:T(8,128)(2,1)S(1)} %collective-permute-done.7), kind=kLoop, calls=%fused_computation.4 | loop fusion | bytes 2097156 | tf_op jit(solution)/shard_map/dynamic_update_slice | solution.py:125
  (23 shorter events, 0.1 us)
Async XLA Ops:
  0.0 28.0 %collective-permute-start.3 = (bf16[12,256,256]{2,1,0:T(8,128)(2,1)}, bf16[12,256,256]{2,1,0:T(8,128)(2,1)}, u32[]{:S(2)}, u32[]{:S(2)}) collective-permute-start(bf16[12,256,256]{2,1,0:T(8,128)(2,1)} %left_ref.3), channel_id=1, source_target_pairs={{0,1},{1,0},{2,3},{3,2},{4,5},{5,4},{6,7},{7,6},{8,9},{9,8},{10,11... | collective-permute-start | bytes 4718600 | tf_op jit(solution)/shard_map/ppermute | solution.py:96
  0.0 28.0 %collective-permute-start.4 = (bf16[12,256,256]{2,1,0:T(8,128)(2,1)}, bf16[12,256,256]{2,1,0:T(8,128)(2,1)}, u32[]{:S(2)}, u32[]{:S(2)}) collective-permute-start(bf16[12,256,256]{2,1,0:T(8,128)(2,1)} %right_ref.3), channel_id=1, source_target_pairs={{0,1},{1,0},{2,3},{3,2},{4,5},{5,4},{6,7},{7,6},{8,9},{9,8},{10,11... | collective-permute-start | bytes 4718600 | tf_op jit(solution)/shard_map/ppermute | solution.py:97
  0.5 6.3 %copy-start.1 = (s32[4]{0:T(128)S(1)}, s32[4]{0:T(128)}, u32[]{:S(2)}) copy-start(s32[4]{0:T(128)} %constant.37.clone) | copy-start | bytes 52
  0.5 9.3 %copy-start = (s32[4]{0:T(128)S(1)}, s32[4]{0:T(128)}, u32[]{:S(2)}) copy-start(s32[4]{0:T(128)} %constant.38.clone) | copy-start | bytes 52
  2.2 11.0 %copy-start.3 = (bf16[8,256,256]{2,1,0:T(8,128)(2,1)}, bf16[8,256,256]{2,1,0:T(8,128)(2,1)S(1)}, u32[]{:S(2)}) copy-start(bf16[8,256,256]{2,1,0:T(8,128)(2,1)S(1)} %get-tuple-element.14.sa) | copy-start | bytes 3145732
  2.2 8.7 %collective-permute-start = (bf16[8,256,256]{2,1,0:T(8,128)(2,1)S(1)}, bf16[8,256,256]{2,1,0:T(8,128)(2,1)}, u32[]{:S(2)}, u32[]{:S(2)}) collective-permute-start(bf16[8,256,256]{2,1,0:T(8,128)(2,1)S(1)} %get-tuple-element.13), channel_id=1, source_target_pairs={{0,1},{1,0},{2,3},{3,2},{4,5},{5,4},{6,7},{7,6},{8,9},{9,8},{10,11... | collective-permute-start | bytes 3145736 | tf_op jit(solution)/shard_map/ppermute | solution.py:93
  2.3 38.6 %collective-permute-start.5 = (bf16[8,256,256]{2,1,0:T(8,128)(2,1)S(1)}, bf16[8,256,256]{2,1,0:T(8,128)(2,1)S(1)}, u32[]{:S(2)}, u32[]{:S(2)}) collective-permute-start(bf16[8,256,256]{2,1,0:T(8,128)(2,1)S(1)} %get-tuple-element.13), channel_id=1, source_target_pairs={{1,2},{3,4},{5,6},{7,8},{9,10},{11,12},{13,14},{2,1},{4,3},{6,5},{... | collective-permute-start | bytes 3145736 | tf_op jit(solution)/shard_map/ppermute | solution.py:91
  4.8 36.1 %collective-permute-start.6 = (bf16[8,256,256]{2,1,0:T(8,128)(2,1)S(1)}, bf16[8,256,256]{2,1,0:T(8,128)(2,1)}, u32[]{:S(2)}, u32[]{:S(2)}) collective-permute-start(bf16[8,256,256]{2,1,0:T(8,128)(2,1)S(1)} %get-tuple-element.14.sa), channel_id=1, source_target_pairs={{1,3},{3,5},{5,7},{7,9},{9,11},{11,13},{13,15},{2,0},{4,2},{6,4},{... | collective-permute-start | bytes 3145736 | tf_op jit(solution)/shard_map/ppermute | solution.py:92
  11.0 15.9 %copy-start.6 = (s32[12]{0:T(128)S(1)}, s32[12]{0:T(128)}, u32[]{:S(2)}) copy-start(s32[12]{0:T(128)} %deltas_ref.3) | copy-start | bytes 148
  11.0 15.9 %collective-permute-start.2 = (s32[1]{0:T(128)}, s32[1]{0:T(128)}, u32[]{:S(2)}, u32[]{:S(2)}) collective-permute-start(s32[1]{0:T(128)} %param.11), channel_id=1, source_target_pairs={{0,1},{1,0},{2,3},{3,2},{4,5},{5,4},{6,7},{7,6},{8,9},{9,8},{10,11... | collective-permute-start | bytes 20 | tf_op jit(solution)/shard_map/ppermute | solution.py:99
  26.8 1.2 %collective-permute-start.1 = (s32[12]{0:T(128)S(1)}, s32[12]{0:T(128)S(1)}, u32[]{:S(2)}, u32[]{:S(2)}) collective-permute-start(s32[12]{0:T(128)S(1)} %copy-done.6), channel_id=1, source_target_pairs={{0,1},{1,0},{2,3},{3,2},{4,5},{5,4},{6,7},{7,6},{8,9},{9,8},{10,11... | collective-permute-start | bytes 152 | tf_op jit(solution)/shard_map/ppermute | solution.py:98
  28.0 0.5 copy-start.7
  40.9 1.0 %copy-start.5 = (bf16[8,256,256]{2,1,0:T(8,128)(2,1)}, bf16[8,256,256]{2,1,0:T(8,128)(2,1)S(1)}, u32[]{:S(2)}) copy-start(bf16[8,256,256]{2,1,0:T(8,128)(2,1)S(1)} %collective-permute-done.5.sa) | copy-start | bytes 3145732
  49.3 33.8 %collective-permute-start.7 = (bf16[8,256,256]{2,1,0:T(8,128)(2,1)}, bf16[8,256,256]{2,1,0:T(8,128)(2,1)S(1)}, u32[]{:S(2)}, u32[]{:S(2)}) collective-permute-start(bf16[8,256,256]{2,1,0:T(8,128)(2,1)} %bitcast.13), channel_id=1, source_target_pairs={{0,1},{1,0},{2,3},{3,2},{4,5},{5,4},{6,7},{7,6},{8,9},{9,8},{10,11... | collective-permute-start | bytes 3145736 | tf_op jit(solution)/shard_map/ppermute | solution.py:121
  81.8 1.2 %copy-start.4 = (bf16[2048,256]{1,0:T(8,128)(2,1)S(1)}, bf16[2048,256]{1,0:T(8,128)(2,1)}, u32[]{:S(2)}) copy-start(bf16[2048,256]{1,0:T(8,128)(2,1)} %shard_map.75) | copy-start | bytes 3145732
  83.1 1.3 %copy-start.2 = (bf16[1,16,256,256]{3,2,1,0:T(8,128)(2,1)}, bf16[1,16,256,256]{3,2,1,0:T(8,128)(2,1)S(1)}, u32[]{:S(2)}) copy-start(bf16[1,16,256,256]{3,2,1,0:T(8,128)(2,1)S(1)} %constant_dynamic-update-slice_fusion) | copy-start | bytes 6291460
